TPU v7x, 256 devices: a whole 4x4x8 slice. The times are simulated.
256 devices in a mesh: expert: 16 (over x, y), dp: 16 (over z, core).
Axes of the slice: x: 4, y: 4, z: 8, core: 2. Of those that a mesh axis runs over, the one named last changes fastest.
Arguments:
- tokens: bfloat16 [4096, 4096], P(('expert', 'dp')), may hold values from -6 to 6
- grad_out: bfloat16 [4096, 4096], P(('expert', 'dp')), may hold values from -6 to 6
- gate_values: bfloat16 [4096, 2], P(('expert', 'dp')), may hold values from 0.099609375 to 1
- routes: int32 [4096, 2], P(('expert', 'dp')), may hold values from 0 to 31, all different within a row; in each aligned block of 16 rows (0 to 15, 16 to 31, ...) at most 2 rows name the same one
- gate_weight: bfloat16 [32, 1536, 4096], P('expert', 'dp'), may hold values from -0.09375 to 0.09375
- up_weight: bfloat16 [32, 1536, 4096], P('expert', 'dp'), may hold values from -0.09375 to 0.09375
- down_weight: bfloat16 [32, 1536, 4096], P('expert', 'dp'), may hold values from -0.15625 to 0.15625
Outputs:
- grad_tokens: bfloat16 [4096, 4096], P(('expert', 'dp'))
- grad_gates: float32 [4096, 2], P(('expert', 'dp'))
- grad_gate_weight: bfloat16 [32, 1536, 4096], P('expert', 'dp')
- grad_up_weight: bfloat16 [32, 1536, 4096], P('expert', 'dp')
- grad_down_weight: bfloat16 [32, 1536, 4096], P('expert', 'dp')
Inputs may be any that keep to these rules, and one draw needn't show every extreme that they name: `routes`: each row names 2 different experts. In each aligned block of 16 rows (the rows of one device) no expert is named by more than 2 rows, a bound that some block reaches.
All inputs are finite; a program needn't handle non-finite values.
Results may differ from a plain program's by a relative error of at most 0.019.
Values may be sent and summed in bfloat16 or wider, within the bound.
No kernel may reach another device: no remote copies, remote signals or barrier semaphores. Data moves between devices by JAX's collectives and lax.ppermute only.
A program may use at most 128 MiB of HBM per device.

v0:
```python
import jax
import jax.numpy as jnp
from jax import lax
from jax.sharding import PartitionSpec as P


def per_device(tokens, grad_out, gate_values, routes, gate_weight, up_weight, down_weight):
    tok_rows, model_width = tokens.shape
    chosen = routes.shape[1]
    local_experts = gate_weight.shape[0]
    groups = lax.axis_size("expert")
    replicas = lax.axis_size("dp")
    experts_all = local_experts * groups
    capacity = 2 * tok_rows * chosen // experts_all
    slot_count = experts_all * capacity
    flat_routes = routes.reshape(-1)
    onehot = (flat_routes[:, None] == jnp.arange(experts_all, dtype=jnp.int32)[None, :]).astype(
        jnp.int32
    )
    earlier = jnp.cumsum(onehot, axis=0) - onehot
    slot_rank = jnp.sum(earlier * onehot, axis=1)
    owner_col = flat_routes // local_experts
    local_id = flat_routes % local_experts
    slot_index = (local_id * groups + owner_col) * capacity + slot_rank
    placing = (jnp.arange(slot_count, dtype=jnp.int32)[:, None] == slot_index[None, :]).astype(
        jnp.float32
    )
    token_map = jnp.sum(placing.reshape(slot_count, tok_rows, chosen), axis=2).astype(jnp.bfloat16)
    slot_gates = jnp.dot(
        placing.astype(jnp.bfloat16), gate_values.reshape(-1), preferred_element_type=jnp.float32
    ).astype(jnp.bfloat16)
    x_slots = jnp.dot(token_map, tokens, preferred_element_type=jnp.float32).astype(jnp.bfloat16)
    dy_slots = jnp.dot(token_map, grad_out, preferred_element_type=jnp.float32).astype(jnp.bfloat16)
    block_shape = (local_experts, groups, capacity, model_width)
    arrived = (
        lax.all_to_all(
            x_slots.reshape(block_shape), "expert", split_axis=1, concat_axis=1, tiled=True
        ),
        lax.all_to_all(
            dy_slots.reshape(block_shape), "expert", split_axis=1, concat_axis=1, tiled=True
        ),
        lax.all_to_all(
            slot_gates.reshape(block_shape[:3]), "expert", split_axis=1, concat_axis=1, tiled=True
        ),
    )
    x_rows, dy_rows, gate_rows = (
        lax.all_gather(arrived[0], "dp", axis=2, tiled=True),
        lax.all_gather(arrived[1], "dp", axis=2, tiled=True),
        lax.all_gather(arrived[2], "dp", axis=2, tiled=True),
    )
    row_total = groups * replicas * capacity
    inputs = x_rows.reshape(local_experts, row_total, model_width)
    upstream = dy_rows.reshape(local_experts, row_total, model_width)
    weighting = gate_rows.reshape(local_experts, row_total).astype(jnp.float32)[..., None]
    gate_pre = jnp.einsum("lrd,lhd->lrh", inputs, gate_weight, preferred_element_type=jnp.float32)
    up_pre = jnp.einsum("lrd,lhd->lrh", inputs, up_weight, preferred_element_type=jnp.float32)
    back_hidden = jnp.einsum(
        "lrd,lhd->lrh", upstream, down_weight, preferred_element_type=jnp.float32
    )
    sigmoid_gate = jax.nn.sigmoid(gate_pre)
    activated = gate_pre * sigmoid_gate
    hidden = activated * up_pre
    gate_part = jnp.sum(back_hidden * hidden, axis=2)
    scaled = weighting * back_hidden
    grad_gate_pre = (
        scaled * up_pre * sigmoid_gate * (1.0 + gate_pre * (1.0 - sigmoid_gate))
    ).astype(jnp.bfloat16)
    grad_up_pre = (scaled * activated).astype(jnp.bfloat16)
    weighted_hidden = (weighting * hidden).astype(jnp.bfloat16)
    input_part = jnp.einsum(
        "lrh,lhd->lrd", grad_gate_pre, gate_weight, preferred_element_type=jnp.float32
    )
    input_part = input_part + jnp.einsum(
        "lrh,lhd->lrd", grad_up_pre, up_weight, preferred_element_type=jnp.float32
    )
    grad_gate_weight = jnp.einsum(
        "lrh,lrd->lhd", grad_gate_pre, inputs, preferred_element_type=jnp.float32
    ).astype(jnp.bfloat16)
    grad_up_weight = jnp.einsum(
        "lrh,lrd->lhd", grad_up_pre, inputs, preferred_element_type=jnp.float32
    ).astype(jnp.bfloat16)
    grad_down_weight = jnp.einsum(
        "lrh,lrd->lhd", weighted_hidden, upstream, preferred_element_type=jnp.float32
    ).astype(jnp.bfloat16)
    part_shape = (local_experts, groups, replicas * capacity, model_width)
    summed = lax.psum_scatter(
        input_part.reshape(part_shape).astype(jnp.bfloat16), "dp", scatter_dimension=2, tiled=True
    )
    returned = lax.all_to_all(summed, "expert", split_axis=1, concat_axis=1, tiled=True)
    returned = returned.reshape(slot_count, model_width)
    grad_tokens = lax.dot_general(
        token_map, returned, (((0,), (0,)), ((), ())), preferred_element_type=jnp.float32
    ).astype(jnp.bfloat16)
    gate_share = gate_part.reshape(local_experts, groups, replicas * capacity)
    gate_total = lax.psum(gate_share, "dp")
    own_gates = lax.dynamic_slice_in_dim(gate_total, lax.axis_index("dp") * capacity, capacity, 2)
    gate_back = lax.all_to_all(
        own_gates, "expert", split_axis=1, concat_axis=1, tiled=True
    ).reshape(slot_count)
    grad_gates = jnp.dot(gate_back, placing, precision=lax.Precision.HIGHEST).reshape(
        tok_rows, chosen
    )
    return (grad_tokens, grad_gates, grad_gate_weight, grad_up_weight, grad_down_weight)


def solution(mesh):
    return jax.shard_map(
        per_device,
        mesh=mesh,
        in_specs=(
            P(("expert", "dp"), None),
            P(("expert", "dp"), None),
            P(("expert", "dp"), None),
            P(("expert", "dp"), None),
            P("expert", "dp", None),
            P("expert", "dp", None),
            P("expert", "dp", None),
        ),
        out_specs=(
            P(("expert", "dp"), None),
            P(("expert", "dp"), None),
            P("expert", "dp", None),
            P("expert", "dp", None),
            P("expert", "dp", None),
        ),
        check_vma=False,
    )
```

profile of v0, /device:TPU:8, one launch (start us, length us, event | category | flops | bytes accessed | tf_op | source)
XLA Modules:
  0.0 287.3 jit_solution(16650401668262213078)
XLA Ops:
  7.2 0.9 copy.82
  8.1 0.1 eq.53
  8.3 0.2 select_reduce_fusion
  8.6 0.1 copy.87
  8.8 1.2 convolution_convert_fusion.3
  10.0 0.3 reshape.143
  10.4 0.5 copy.95
  10.8 17.3 %all_to_all.25 = bf16[2,16,2,4096]{3,2,0,1:T(2,128)(2,1)S(1)} all-to-all(bf16[2,16,2,4096]{3,2,0,1:T(2,128)(2,1)S(1)} %copy.95), channel_id=1, replica_groups=mesh['expert'=16,'dp'=16] {'expert'}, dimensions={1} | all-to-all | bytes 1048576 | tf_op jit(solution)/shard_map/all_to_all | solution.py:36
  28.2 1.1 copy.96
  29.3 1.2 convolution_convert_fusion.4
  30.5 0.3 reshape.141
  30.9 0.5 copy.92
  31.4 13.7 %all_to_all.26 = bf16[2,16,2,4096]{3,2,0,1:T(2,128)(2,1)S(1)} all-to-all(bf16[2,16,2,4096]{3,2,0,1:T(2,128)(2,1)S(1)} %copy.92), channel_id=1, replica_groups=mesh['expert'=16,'dp'=16] {'expert'}, dimensions={1} | all-to-all | bytes 1048576 | tf_op jit(solution)/shard_map/all_to_all | solution.py:39
  45.0 1.1 copy.93
  46.2 0.1 copy.88
  46.3 0.1 reshape.149
  46.4 0.1 fusion
  46.5 0.1 reshape.140
  46.7 10.8 %all_to_all.27 = bf16[2,16,2]{2,0,1:T(2,128)(2,1)S(1)} all-to-all(bf16[2,16,2]{2,0,1:T(2,128)(2,1)S(1)} %copy.89), channel_id=1, replica_groups=mesh['expert'=16,'dp'=16] {'expert'}, dimensions={1} | all-to-all | bytes 256 | tf_op jit(solution)/shard_map/all_to_all | solution.py:42
  57.5 0.1 copy.90
  57.6 20.6 %all_gather.9 = bf16[2,16,32]{1,0,2:T(2,128)(2,1)S(1)} all-gather(bf16[2,16,2]{1,0,2:T(2,128)(2,1)S(1)} %copy.90), channel_id=1, replica_groups=mesh['expert'=16,'dp'=16] {'dp'}, dimensions={2}, use_global_device_ids=true | all-gather | bytes 2176 | tf_op jit(solution)/shard_map/all_gather | solution.py:49
  78.2 0.1 copy.91
  78.3 0.1 reshape.148
  78.4 7.3 %all-gather.5.cloned.1.call-done = bf16[2,16,32,4096]{3,1,0,2:T(8,128)(2,1)} async-done(((bf16[2,16,2,4096]{3,1,0,2:T(8,128)(2,1)}), bf16[2,16,32,4096]{3,1,0,2:T(8,128)(2,1)}) %all-gather.5.cloned.1.call-update) | async-done | bytes 8388624 | tf_op jit(solution)/shard_map/all_gather | solution.py:47
  85.7 11.2 %copy.97 = bf16[2,16,32,4096]{3,2,1,0:T(8,128)(2,1)} copy(bf16[2,16,32,4096]{3,1,0,2:T(8,128)(2,1)} %all-gather.5.cloned.1.call-done) | data formatting | bytes 16777216 | tf_op jit(solution)/shard_map/all_gather | solution.py:47
  96.9 6.6 %fusion.23 = f32[2,512,96]{1,2,0:T(8,128)S(1)} fusion(bf16[2,512,4096]{2,1,0:T(8,128)(2,1)} %bitcast.33, bf16[2,96,4096]{2,1,0:T(8,128)(2,1)S(1)} %copy-done), kind=kOutput, calls=%fused_computation.55 | convolution fusion | flops 805306368 | bytes 10354688 | tf_op jit(solution)/shard_map/lrd,lhd->lrh/dot_general | solution.py:55
  103.5 2.7 fusion.22
  106.2 36.3 %all-gather.3.cloned.1.call-done = bf16[2,16,32,4096]{3,1,0,2:T(8,128)(2,1)} async-done(((bf16[2,16,2,4096]{3,1,0,2:T(8,128)(2,1)}), bf16[2,16,32,4096]{3,1,0,2:T(8,128)(2,1)}) %all-gather.3.cloned.1.call-update) | async-done | bytes 8388624 | tf_op jit(solution)/shard_map/all_gather | solution.py:48
  142.5 11.5 %copy.94 = bf16[2,16,32,4096]{3,2,1,0:T(8,128)(2,1)} copy(bf16[2,16,32,4096]{3,1,0,2:T(8,128)(2,1)} %all-gather.3.cloned.1.call-done) | data formatting | bytes 16777216 | tf_op jit(solution)/shard_map/all_gather | solution.py:48
  154.0 6.2 %multiply_reduce_fusion = (f32[2,512]{1,0:T(2,128)S(1)}, bf16[2,512,96]{1,2,0:T(8,128)(2,1)S(1)}, bf16[2,512,96]{1,2,0:T(8,128)(2,1)S(1)}) fusion(f32[2,512,96]{1,2,0:T(8,128)S(1)} %fusion.22, f32[2,512,96]{1,2,0:T(8,128)S(1)} %fusion.23, f32[2,512]{1,0:T(2,128)S(1)} %reshape.148, bf16[2,512,4096]{2,1,0:T(8,128)(2,1)} %bitcast.37, ...), kind=kOutput, calls=%fused_computation.10 | convolution fusion | flops 806976512 | bytes 11149312 | tf_op jit(solution)/shard_map/lrd,lhd->lrh/dot_general | solution.py:57
  160.2 8.1 %fusion.24 = f32[2,512,4096]{2,1,0:T(8,128)} fusion(bf16[2,512,96]{1,2,0:T(8,128)(2,1)S(1)} %get-tuple-element.6, bf16[2,96,4096]{2,1,0:T(8,128)(2,1)S(1)} %copy-done), kind=kOutput, calls=%fused_computation.56 | convolution fusion | flops 805306368 | bytes 18546688 | tf_op jit(solution)/shard_map/lrh,lhd->lrd/dot_general | solution.py:70
  168.3 11.4 %add_convert_fusion = bf16[2,512,4096]{2,1,0:T(8,128)(2,1)} fusion(f32[2,512,4096]{2,1,0:T(8,128)} %fusion.24, bf16[2,512,96]{1,2,0:T(8,128)(2,1)S(1)} %get-tuple-element.7, bf16[2,96,4096]{2,1,0:T(8,128)(2,1)S(1)} %copy-done.4), kind=kOutput, calls=%fused_computation | convolution fusion | flops 813694976 | bytes 26935296 | tf_op jit(solution)/shard_map/lrh,lhd->lrd/dot_general | solution.py:73
  179.8 11.4 %copy.98 = bf16[2,16,32,4096]{3,1,0,2:T(8,128)(2,1)} copy(bf16[2,16,32,4096]{3,2,1,0:T(8,128)(2,1)} %bitcast.39) | data formatting | bytes 16777216 | tf_op jit(solution)/shard_map/convert_element_type | solution.py:87
  191.4 46.9 %psum.7 = f32[2,16,32]{2,1,0:T(8,128)S(1)} all-reduce(f32[2,16,32]{2,1,0:T(8,128)S(1)} %reshape.146), channel_id=1, replica_groups=mesh['expert'=16,'dp'=16] {'dp'}, use_global_device_ids=true, to_apply=%region_5.6 | all-reduce | flops 1024 | bytes 8192 | tf_op jit(solution)/shard_map/psum | solution.py:95
  238.4 0.6 copy.101
  239.0 7.3 %all-to-all-start.4 = ((f32[2,16,2]{2,0,1:T(2,128)}), f32[2,16,2]{2,0,1:T(2,128)S(1)}, u32[]{:S(2)}, u32[]{:S(2)}) async-start(f32[2,16,2]{2,0,1:T(2,128)} %copy.101), calls=%async_computation.5 | async-start | bytes 32768 | tf_op jit(solution)/shard_map/all_to_all | solution.py:97
  246.3 6.2 %convolution_convert_fusion = bf16[2,96,4096]{2,1,0:T(8,128)(2,1)} fusion(bf16[2,512,4096]{2,1,0:T(8,128)(2,1)} %bitcast.38, f32[2,512]{1,0:T(2,128)S(1)} %reshape.148, f32[2,512,96]{1,2,0:T(8,128)S(1)} %fusion.22, f32[2,512,96]{1,2,0:T(8,128)S(1)} %fusion.23), kind=kOutput, calls=%fused_computation.1 | convolution fusion | flops 806780928 | bytes 10752000 | tf_op jit(solution)/shard_map/lrh,lrd->lhd/dot_general | solution.py:82
  252.5 6.2 %convolution_convert_fusion.2 = bf16[2,96,4096]{2,1,0:T(8,128)(2,1)} fusion(bf16[2,512,96]{1,2,0:T(8,128)(2,1)S(1)} %get-tuple-element.6, bf16[2,512,4096]{2,1,0:T(8,128)(2,1)} %bitcast.34), kind=kOutput, calls=%fused_computation.3 | convolution fusion | flops 806092800 | bytes 10158080 | tf_op jit(solution)/shard_map/lrh,lrd->lhd/dot_general | solution.py:76
  258.6 2.4 reduce-scatter.2.cloned.1.call-done
  261.0 2.4 copy.99
  263.4 7.1 %all-to-all-start.3 = ((bf16[2,16,2,4096]{3,2,0,1:T(2,128)(2,1)}), bf16[2,16,2,4096]{3,2,0,1:T(2,128)(2,1)S(1)}, u32[]{:S(2)}, u32[]{:S(2)}) async-start(bf16[2,16,2,4096]{3,2,0,1:T(2,128)(2,1)} %copy.99), calls=%async_computation.4 | async-start | bytes 1048576 | tf_op jit(solution)/shard_map/all_to_all | solution.py:89
  270.5 6.1 %convolution_convert_fusion.1 = bf16[2,96,4096]{2,1,0:T(8,128)(2,1)} fusion(bf16[2,512,96]{1,2,0:T(8,128)(2,1)S(1)} %get-tuple-element.7, bf16[2,512,4096]{2,1,0:T(8,128)(2,1)} %bitcast.35), kind=kOutput, calls=%fused_computation.2 | convolution fusion | flops 806092800 | bytes 10158080 | tf_op jit(solution)/shard_map/lrh,lrd->lhd/dot_general | solution.py:79
  276.6 0.1 reshape.151
  276.7 0.8 fusion.6
  277.5 1.8 all-to-all-done.3
  279.3 0.4 copy.100
  279.7 0.2 reshape.145
  279.9 0.9 convolution_convert_fusion.5
  (33 shorter events, 0.8 us)
Async XLA Ops:
  7.2 89.7 %copy-start = (bf16[2,96,4096]{2,1,0:T(8,128)(2,1)S(1)}, bf16[2,96,4096]{2,1,0:T(8,128)(2,1)}, u32[]{:S(2)}) copy-start(bf16[2,96,4096]{2,1,0:T(8,128)(2,1)} %param.11) | copy-start | bytes 4718596
  7.2 39.0 %copy-start.6 = (bf16[16,2]{0,1:T(2,128)(2,1)S(1)}, bf16[16,2]{0,1:T(2,128)(2,1)}, u32[]{:S(2)}) copy-start(bf16[16,2]{0,1:T(2,128)(2,1)} %param.9) | copy-start | bytes 196
  7.2 78.5 %all-gather.5.cloned.1.call-start = ((), (), s32[]{:S(2)}) async-start(), calls=%async_computation.7 | async-start | bytes 8912896 | tf_op jit(solution)/shard_map/all_gather | solution.py:47
  29.3 113.3 %all-gather.3.cloned.1.call-start = ((), (), s32[]{:S(2)}) async-start(), calls=%async_computation.6 | async-start | bytes 8912896 | tf_op jit(solution)/shard_map/all_gather | solution.py:48
  46.1 214.9 %reduce-scatter.2.cloned.1.call-start = ((), (), s32[]{:S(2)}) async-start(), calls=%async_computation.8 | async-start | bytes 8912896 | tf_op jit(solution)/shard_map/reduce_scatter | solution.py:86
  96.9 6.6 %copy-start.2 = (bf16[2,16,32,4096]{3,2,1,0:T(8,128)(2,1)S(1)}, bf16[2,16,32,4096]{3,2,1,0:T(8,128)(2,1)}, u32[]{:S(2)}) copy-start(bf16[2,16,32,4096]{3,2,1,0:T(8,128)(2,1)} %copy.97) | copy-start | bytes 25165828
  96.9 6.6 %copy-start.3 = (bf16[2,96,4096]{2,1,0:T(8,128)(2,1)S(1)}, bf16[2,96,4096]{2,1,0:T(8,128)(2,1)}, u32[]{:S(2)}) copy-start(bf16[2,96,4096]{2,1,0:T(8,128)(2,1)} %param.12) | copy-start | bytes 4718596
  142.5 11.5 %copy-start.5 = (bf16[2,96,4096]{2,1,0:T(8,128)(2,1)S(1)}, bf16[2,96,4096]{2,1,0:T(8,128)(2,1)}, u32[]{:S(2)}) copy-start(bf16[2,96,4096]{2,1,0:T(8,128)(2,1)} %param.13) | copy-start | bytes 4718596
  160.2 8.1 %copy-start.4 = (bf16[2,96,4096]{2,1,0:T(8,128)(2,1)S(1)}, bf16[2,96,4096]{2,1,0:T(8,128)(2,1)}, u32[]{:S(2)}) copy-start(bf16[2,96,4096]{2,1,0:T(8,128)(2,1)} %param.12) | copy-start | bytes 4718596
  239.0 24.4 %all-to-all-start.4 = ((f32[2,16,2]{2,0,1:T(2,128)}), f32[2,16,2]{2,0,1:T(2,128)S(1)}, u32[]{:S(2)}, u32[]{:S(2)}) async-start(f32[2,16,2]{2,0,1:T(2,128)} %copy.101), calls=%async_computation.5 | async-start | bytes 32768 | tf_op jit(solution)/shard_map/all_to_all | solution.py:97
  263.4 15.8 %all-to-all-start.3 = ((bf16[2,16,2,4096]{3,2,0,1:T(2,128)(2,1)}), bf16[2,16,2,4096]{3,2,0,1:T(2,128)(2,1)S(1)}, u32[]{:S(2)}, u32[]{:S(2)}) async-start(bf16[2,16,2,4096]{3,2,0,1:T(2,128)(2,1)} %copy.99), calls=%async_computation.4 | async-start | bytes 1048576 | tf_op jit(solution)/shard_map/all_to_all | solution.py:89
  270.5 10.2 %copy-start.1 = (bf16[2,96,4096]{2,1,0:T(8,128)(2,1)S(1)}, bf16[2,96,4096]{2,1,0:T(8,128)(2,1)}, u32[]{:S(2)}) copy-start(bf16[2,96,4096]{2,1,0:T(8,128)(2,1)} %param.11) | copy-start | bytes 4718596
Sparse Core Ops, SparseCore 0:
  29.4 56.2 all-gather.4
  88.1 54.3 all-gather.2
  191.4 69.5 reduce-scatter.1
where the time goes:
time: 288 us; the launch traced here: 287 us
  blocking collectives  109 us (38%)
  matrix products  57.6 us (20%)
  waiting for transfers between devices  47.8 us (17%)
  local copies, waits for them, and re-layouts  43.6 us (15%)
  starting transfers between devices  14.5 us (5%)
  between operations  13.9 us (5%)
    psum x1, blocking collectives, per_device(): gate_total = lax.psum(gate_share, 'dp')  46.9 us
    all_gather x1, waiting for transfers between devices, per_device(): lax.all_gather(arrived[1], 'dp', axis=2, tiled=True)  36.3 us
    all_gather x1, blocking collectives, per_device(): lax.all_gather(arrived[2], 'dp', axis=2, tiled=True)  20.6 us
    all_to_all x1, blocking collectives, per_device(): lax.all_to_all(x_slots.reshape(block_shape), 'expert', split_axis=1, conc...  17.3 us
    all_to_all x1, blocking collectives, per_device(): lax.all_to_all(dy_slots.reshape(block_shape), 'expert', split_axis=1, con...  13.7 us
    all_gather x1, local copies, waits for them, and re-layouts, per_device(): lax.all_gather(arrived[1], 'dp', axis=2, tiled=True)  11.5 us
    convert_element_type x1, local copies, waits for them, and re-layouts, per_device(): input_part.reshape(part_shape).astype(jnp.bfloat16)  11.4 us
    dot_general x1, matrix products, per_device(): jnp.einsum('lrh,lhd->lrd', grad_up_pre, up_weight, preferred_element_type...  11.4 us
  transfers between devices with their start and end apart: 5, of which 4 were waited for; matrix products, arithmetic and copies ran while one was open for 16% of the time, Pallas kernels for 0%

commit v1 on v0

v1 whole, which is shorter than its diff:
```python
import jax
import jax.numpy as jnp
from jax import lax
from jax.sharding import Mesh
from jax.sharding import PartitionSpec as P

CORES = 2
PAD = 128


def per_device(tokens, grad_out, gate_values, routes, gate_weight, up_weight, down_weight):
    f32, bf16 = jnp.float32, jnp.bfloat16
    tok_rows, model_width = tokens.shape
    chosen = routes.shape[1]
    local_experts = gate_weight.shape[0]
    groups = lax.axis_size("expert")
    n_z = lax.axis_size("z")
    n_core = lax.axis_size("core")
    experts_all = local_experts * groups
    capacity = 2 * tok_rows * chosen // experts_all
    slot_count = experts_all * capacity
    block_rows = groups * capacity
    gathered_rows = n_core * n_z * block_rows
    width = 2 * model_width + PAD
    back_width = model_width + PAD

    flat_routes = routes.reshape(-1)
    onehot = (flat_routes[:, None] == jnp.arange(experts_all, dtype=jnp.int32)[None, :]).astype(
        jnp.int32
    )
    earlier = jnp.cumsum(onehot, axis=0) - onehot
    slot_rank = jnp.sum(earlier * onehot, axis=1)
    owner_col = flat_routes // local_experts
    local_id = flat_routes % local_experts
    slot_index = (local_id * groups + owner_col) * capacity + slot_rank
    placing = (jnp.arange(slot_count, dtype=jnp.int32)[:, None] == slot_index[None, :]).astype(f32)
    token_map = jnp.sum(placing.reshape(slot_count, tok_rows, chosen), axis=2).astype(bf16)
    slot_gates = jnp.dot(
        placing.astype(bf16), gate_values.reshape(-1), preferred_element_type=f32
    ).astype(bf16)
    x_slots = jnp.dot(token_map, tokens, preferred_element_type=f32).astype(bf16)
    dy_slots = jnp.dot(token_map, grad_out, preferred_element_type=f32).astype(bf16)
    gate_cols = jnp.concatenate(
        [slot_gates[:, None], jnp.zeros((slot_count, PAD - 1), bf16)], axis=1
    )
    payload = jnp.concatenate([x_slots, dy_slots, gate_cols], axis=1)
    payload = payload.reshape(local_experts, groups, capacity, width)

    backs, ggw, guw, gdw = [], [], [], []
    for l in range(local_experts):
        with jax.named_scope(f"expert_{l}"):
            blk = lax.all_to_all(payload[l], "expert", split_axis=0, concat_axis=0, tiled=True)
            blk = blk.reshape(block_rows, width)
            gz = lax.all_gather(blk, "z", axis=0)
            gzc = lax.all_gather(gz, "core", axis=0)
            rows = gzc.reshape(gathered_rows, width)
            inputs = rows[:, :model_width]
            upstream = rows[:, model_width : 2 * model_width]
            weighting = rows[:, 2 * model_width].astype(f32)[:, None]
            gw, uw, dw = gate_weight[l], up_weight[l], down_weight[l]
            gate_pre = jnp.einsum("rd,hd->rh", inputs, gw, preferred_element_type=f32)
            up_pre = jnp.einsum("rd,hd->rh", inputs, uw, preferred_element_type=f32)
            back_hidden = jnp.einsum("rd,hd->rh", upstream, dw, preferred_element_type=f32)
            sigmoid_gate = jax.nn.sigmoid(gate_pre)
            activated = gate_pre * sigmoid_gate
            hidden = activated * up_pre
            gate_part = jnp.sum(back_hidden * hidden, axis=1)
            scaled = weighting * back_hidden
            grad_gate_pre = (
                scaled * up_pre * sigmoid_gate * (1.0 + gate_pre * (1.0 - sigmoid_gate))
            ).astype(bf16)
            grad_up_pre = (scaled * activated).astype(bf16)
            weighted_hidden = (weighting * hidden).astype(bf16)
            input_part = jnp.einsum("rh,hd->rd", grad_gate_pre, gw, preferred_element_type=f32)
            input_part = input_part + jnp.einsum(
                "rh,hd->rd", grad_up_pre, uw, preferred_element_type=f32
            )
            hi = gate_part.astype(bf16)
            lo = (gate_part - hi.astype(f32)).astype(bf16)
            tail = jnp.concatenate(
                [hi[:, None], lo[:, None], jnp.zeros((gathered_rows, PAD - 2), bf16)], axis=1
            )
            back = jnp.concatenate([input_part.astype(bf16), tail], axis=1)
            back = back.reshape(n_core, n_z, block_rows, back_width)
            back = lax.psum_scatter(back, "core", scatter_dimension=0, tiled=True)
            back = lax.psum_scatter(back, "z", scatter_dimension=1, tiled=True)
            backs.append(back.reshape(groups, capacity, back_width))
            ggw.append(
                jnp.einsum("rh,rd->hd", grad_gate_pre, inputs, preferred_element_type=f32).astype(bf16)
            )
            guw.append(
                jnp.einsum("rh,rd->hd", grad_up_pre, inputs, preferred_element_type=f32).astype(bf16)
            )
            gdw.append(
                jnp.einsum("rh,rd->hd", weighted_hidden, upstream, preferred_element_type=f32).astype(
                    bf16
                )
            )

    back_all = jnp.stack(backs)
    returned = lax.all_to_all(back_all, "expert", split_axis=1, concat_axis=1, tiled=True)
    returned = returned.reshape(slot_count, back_width)
    grad_tokens = lax.dot_general(
        token_map,
        returned[:, :model_width],
        (((0,), (0,)), ((), ())),
        preferred_element_type=f32,
    ).astype(bf16)
    gate_back = returned[:, model_width].astype(f32) + returned[:, model_width + 1].astype(f32)
    grad_gates = jnp.dot(gate_back, placing, precision=lax.Precision.HIGHEST).reshape(
        tok_rows, chosen
    )
    return (grad_tokens, grad_gates, jnp.stack(ggw), jnp.stack(guw), jnp.stack(gdw))


def solution(mesh):
    n_expert, n_dp = mesh.devices.shape
    split = Mesh(mesh.devices.reshape(n_expert, n_dp // CORES, CORES), ("expert", "z", "core"))
    rows = P(("expert", "z", "core"), None)
    blocks = P("expert", ("z", "core"), None)
    return jax.shard_map(
        per_device,
        mesh=split,
        in_specs=(rows, rows, rows, rows, blocks, blocks, blocks),
        out_specs=(rows, rows, blocks, blocks, blocks),
        check_vma=False,
    )
```

time: 288 us -> 363 us (1.26)
  waiting for transfers between devices: 47.8 us -> 224 us
  blocking collectives: 109 us -> 31.5 us
  local copies, waits for them, and re-layouts: 43.6 us -> 24.9 us
  other arithmetic: 0.51 us -> 7.53 us
  starting transfers between devices: 14.5 us -> 7.75 us
  matrix products: 57.6 us -> 51.7 us
    reduce_scatter x1 -> x4, waiting for transfers between devices: 2.36 us -> 91 us  [the longest x2 72.8 us: per_device(): back = lax.psum_scatter(back, 'z', scatter_dimension=1, tiled=True)]
    all_gather x2 -> x4, waiting for transfers between devices: 43.6 us -> 127 us  [the longest x2 96.8 us: per_device(): gz = lax.all_gather(blk, 'z', axis=0)]
    psum x1 -> x0, blocking collectives: 46.9 us -> none  [per_device(): gate_total = lax.psum(gate_share, 'dp')]
    all_gather x3 -> x0, local copies, waits for them, and re-layouts: 22.8 us -> none  [the longest x1 11.5 us: per_device(): lax.all_gather(arrived[1], 'dp', axis=2, tiled=True)]
    all_gather x1 -> x0, blocking collectives: 20.6 us -> none  [per_device(): lax.all_gather(arrived[2], 'dp', axis=2, tiled=True)]
    concatenate x0 -> x4, local copies, waits for them, and re-layouts: none -> 16.6 us  [the longest x3 15.8 us: per_device(): back = jnp.concatenate([input_part.astype(bf16), tail], axis=1)]
    convert_element_type x2 -> x4, local copies, waits for them, and re-layouts: 11.5 us -> 0.83 us  [the longest x2 0.42 us: per_device(): lo = (gate_part - hi.astype(f32)).astype(bf16)]
    all_to_all x3 -> x2, blocking collectives: 41.8 us -> 31.5 us  [per_device(): lax.all_to_all(payload[l], 'expert', split_axis=0, concat_axis=0, tiled=T...]
  transfers between devices with their start and end apart: 5 -> 9, of which waited for: 4 -> 8; matrix products, arithmetic and copies ran while one was open for 16% -> 20% of each run, Pallas kernels for 0% -> 0%
where the time goes in v1:
time: 363 us; the launch traced here: 362 us
  waiting for transfers between devices  224 us (62%)
  matrix products  51.7 us (14%)
  blocking collectives  31.5 us (9%)
  local copies, waits for them, and re-layouts  24.9 us (7%)
  between operations  14.6 us (4%)
  starting transfers between devices  7.75 us (2%)
  other arithmetic  7.53 us (2%)
    all_gather x2, waiting for transfers between devices, per_device(): gz = lax.all_gather(blk, 'z', axis=0)  96.8 us
    reduce_scatter x2, waiting for transfers between devices, per_device(): back = lax.psum_scatter(back, 'z', scatter_dimension=1, tiled=True)  72.8 us
    all_to_all x2, blocking collectives, per_device(): lax.all_to_all(payload[l], 'expert', split_axis=0, concat_axis=0, tiled=T...  31.5 us
    all_gather x2, waiting for transfers between devices, per_device(): gzc = lax.all_gather(gz, 'core', axis=0)  30.5 us
    reduce_scatter x2, waiting for transfers between devices, per_device(): back = lax.psum_scatter(back, 'core', scatter_dimension=0, tiled=True)  18.2 us
    concatenate x3, local copies, waits for them, and re-layouts, per_device(): back = jnp.concatenate([input_part.astype(bf16), tail], axis=1)  15.8 us
    dot_general x2, matrix products, per_device(): gate_pre = jnp.einsum('rd,hd->rh', inputs, gw, preferred_element_type=f32)  7.52 us
    dot_general x2, matrix products, per_device(): up_pre = jnp.einsum('rd,hd->rh', inputs, uw, preferred_element_type=f32)  7.46 us
  transfers between devices with their start and end apart: 9, of which 8 were waited for; matrix products, arithmetic and copies ran while one was open for 20% of the time, Pallas kernels for 0%

profile of v1, /device:TPU:8, one launch (start us, length us, event | category | flops | bytes accessed | tf_op | source)
XLA Modules:
  0.0 361.5 jit_solution(12305142287552700891)
XLA Ops:
  7.2 0.8 copy.57
  8.5 0.8 copy.63
  9.8 0.3 convolution_convert_fusion.6
  10.1 1.2 convolution_convert_fusion.7
  11.4 0.8 concatenate.17
  12.5 17.7 %all_to_all.15 = bf16[16,2,8320]{2,1,0:T(2,128)(2,1)S(1)} all-to-all(bf16[16,2,8320]{2,1,0:T(2,128)(2,1)S(1)} %squeeze.28), channel_id=1, replica_groups=mesh['expert'=16,'z'=8,'core'=2] {'expert'}, dimensions={0} | all-to-all | bytes 1064960 | tf_op jit(solution)/shard_map/expert_0/all_to_all | solution.py:52
  30.1 1.0 reshape.205
  31.4 13.8 %all_to_all.16 = bf16[16,2,8320]{2,1,0:T(2,128)(2,1)S(1)} all-to-all(bf16[16,2,8320]{2,1,0:T(2,128)(2,1)S(1)} %squeeze.32), channel_id=1, replica_groups=mesh['expert'=16,'z'=8,'core'=2] {'expert'}, dimensions={0} | all-to-all | bytes 1064960 | tf_op jit(solution)/shard_map/expert_1/all_to_all | solution.py:52
  45.2 1.0 reshape.208
  46.3 40.5 %all-gather.7.cloned.1.call-done = bf16[8,32,8320]{2,1,0:T(8,128)(2,1)} async-done(((bf16[1,32,8320]{2,1,0:T(8,128)(2,1)}), bf16[8,32,8320]{2,1,0:T(8,128)(2,1)}) %all-gather.7.cloned.1.call-update) | async-done | bytes 4259856 | tf_op jit(solution)/shard_map/expert_0/all_gather | solution.py:54
  86.9 56.3 %all-gather.9.cloned.1.call-done = bf16[8,32,8320]{2,1,0:T(8,128)(2,1)} async-done(((bf16[1,32,8320]{2,1,0:T(8,128)(2,1)}), bf16[8,32,8320]{2,1,0:T(8,128)(2,1)}) %all-gather.9.cloned.1.call-update) | async-done | bytes 4259856 | tf_op jit(solution)/shard_map/expert_1/all_gather | solution.py:54
  143.3 26.4 %all-gather.11.cloned.1.call-done = bf16[16,32,8320]{2,1,0:T(8,128)(2,1)} async-done(((bf16[8,32,8320]{2,1,0:T(8,128)(2,1)}), bf16[16,32,8320]{2,1,0:T(8,128)(2,1)}) %all-gather.11.cloned.1.call-update) | async-done | bytes 8519696 | tf_op jit(solution)/shard_map/expert_0/all_gather | solution.py:55
  169.7 1.0 convert_reduce_fusion.1
  170.8 3.8 %fusion.20 = f32[512,96]{0,1:T(8,128)S(1)} fusion(bf16[512,8320]{1,0:T(8,128)(2,1)} %bitcast.81, bf16[2,96,4096]{2,1,0:T(8,128)(2,1)S(1)} %copy-done.2), kind=kOutput, calls=%fused_computation.31 | convolution fusion | flops 402653184 | bytes 5177344 | tf_op jit(solution)/shard_map/expert_0/rd,hd->rh/dot_general | solution.py:61
  174.6 3.7 %fusion.22 = f32[512,96]{0,1:T(8,128)S(1)} fusion(bf16[512,8320]{1,0:T(8,128)(2,1)} %bitcast.82, bf16[2,96,4096]{2,1,0:T(8,128)(2,1)S(1)} %copy-done.3), kind=kOutput, calls=%fused_computation.33 | convolution fusion | flops 402653184 | bytes 5177344 | tf_op jit(solution)/shard_map/expert_0/rd,hd->rh/dot_general | solution.py:62
  178.3 2.1 multiply_reduce_fusion.1
  180.9 2.2 fusion.32
  183.1 3.4 add_convert_fusion.1
  186.6 7.9 %concatenate.20 = bf16[2,8,32,4224]{3,2,1,0:T(8,128)(2,1)} concatenate(bf16[2,8,32,4096]{3,2,1,0:T(8,128)(2,1)} %bitcast.78, bf16[2,8,32,1]{3,2,1,0:T(8,128)(2,1)S(1)} %copy.65, bf16[2,8,32,1]{3,2,1,0:T(8,128)(2,1)S(1)} %copy.66, bf16[2,8,32,126]{3,2,1,0:T(8,128)(2,1)S(1)} %concatenate.19), dimensions={3} | concatenate | bytes 8650752 | tf_op jit(solution)/shard_map/expert_0/concatenate | solution.py:83
  194.5 0.2 reduce-scatter.9.cloned.1.call-start
  194.8 4.0 %all-gather.13.cloned.1.call-done = bf16[16,32,8320]{2,1,0:T(8,128)(2,1)} async-done(((bf16[8,32,8320]{2,1,0:T(8,128)(2,1)}), bf16[16,32,8320]{2,1,0:T(8,128)(2,1)}) %all-gather.13.cloned.1.call-update) | async-done | bytes 8519696 | tf_op jit(solution)/shard_map/expert_1/all_gather | solution.py:55
  198.8 1.0 convert_reduce_fusion
  199.8 3.8 %fusion.14 = f32[512,96]{0,1:T(8,128)S(1)} fusion(bf16[512,8320]{1,0:T(8,128)(2,1)} %bitcast.88, bf16[2,96,4096]{2,1,0:T(8,128)(2,1)S(1)} %copy-done.2), kind=kOutput, calls=%fused_computation.25 | convolution fusion | flops 402653184 | bytes 5177344 | tf_op jit(solution)/shard_map/expert_1/rd,hd->rh/dot_general | solution.py:61
  203.6 3.7 %fusion.16 = f32[512,96]{0,1:T(8,128)S(1)} fusion(bf16[512,8320]{1,0:T(8,128)(2,1)} %bitcast.89, bf16[2,96,4096]{2,1,0:T(8,128)(2,1)S(1)} %copy-done.3), kind=kOutput, calls=%fused_computation.27 | convolution fusion | flops 402653184 | bytes 5177344 | tf_op jit(solution)/shard_map/expert_1/rd,hd->rh/dot_general | solution.py:62
  207.4 2.1 multiply_reduce_fusion
  210.0 2.2 fusion.26
  212.2 3.3 add_convert_fusion
  215.6 7.9 %concatenate.22 = bf16[2,8,32,4224]{3,2,1,0:T(8,128)(2,1)} concatenate(bf16[2,8,32,4096]{3,2,1,0:T(8,128)(2,1)} %bitcast.79, bf16[2,8,32,1]{3,2,1,0:T(8,128)(2,1)S(1)} %copy.67, bf16[2,8,32,1]{3,2,1,0:T(8,128)(2,1)S(1)} %copy.68, bf16[2,8,32,126]{3,2,1,0:T(8,128)(2,1)S(1)} %concatenate.19), dimensions={3} | concatenate | bytes 8650752 | tf_op jit(solution)/shard_map/expert_1/concatenate | solution.py:83
  223.5 0.7 reduce-scatter.7.cloned.1.call-update
  224.3 18.2 %reduce-scatter.9.cloned.1.call-done = bf16[1,8,32,4224]{3,2,1,0:T(8,128)(2,1)} async-done(((bf16[2,8,32,4224]{3,2,1,0:T(8,128)(2,1)}), bf16[1,8,32,4224]{3,2,1,0:T(8,128)(2,1)}) %reduce-scatter.9.cloned.1.call-update) | async-done | bytes 2162704 | tf_op jit(solution)/shard_map/expert_1/reduce_scatter | solution.py:85
  242.6 3.0 fusion.1
  245.7 3.0 fusion.3
  248.7 3.0 fusion
  251.8 3.0 fusion.4
  254.8 3.0 fusion.5
  257.8 1.9 pad_maximum_fusion
  259.8 29.6 %reduce-scatter.7.cloned.1.call-done = bf16[1,1,32,4224]{3,2,1,0:T(8,128)(2,1)} async-done(((bf16[1,8,32,4224]{3,2,1,0:T(8,128)(2,1)}), bf16[1,1,32,4224]{3,2,1,0:T(8,128)(2,1)}) %reduce-scatter.7.cloned.1.call-update) | async-done | bytes 270352 | tf_op jit(solution)/shard_map/expert_0/reduce_scatter | solution.py:86
  289.4 1.1 reshape.207
  290.4 43.2 %reduce-scatter.11.cloned.1.call-done = bf16[1,1,32,4224]{3,2,1,0:T(8,128)(2,1)} async-done(((bf16[1,8,32,4224]{3,2,1,0:T(8,128)(2,1)}), bf16[1,1,32,4224]{3,2,1,0:T(8,128)(2,1)}) %reduce-scatter.11.cloned.1.call-update) | async-done | bytes 270352 | tf_op jit(solution)/shard_map/expert_1/reduce_scatter | solution.py:86
  333.6 1.1 reshape.210
  334.6 1.6 pad_maximum_fusion.3
  336.2 7.3 %all-to-all-start.2 = ((bf16[2,16,2,4224]{3,2,0,1:T(2,128)(2,1)}), bf16[2,16,2,4224]{3,2,0,1:T(2,128)(2,1)S(1)}, u32[]{:S(2)}, u32[]{:S(2)}) async-start(bf16[2,16,2,4224]{3,2,0,1:T(2,128)(2,1)} %pad_maximum_fusion.3), calls=%async_computation.6 | async-start | bytes 1081344 | tf_op jit(solution)/shard_map/all_to_all | solution.py:101
  343.5 3.0 fusion.2
  346.5 1.3 pad_maximum_fusion.1
  347.8 4.5 %all-to-all-done.2 = bf16[2,16,2,4224]{3,2,0,1:T(2,128)(2,1)S(1)} async-done(((bf16[2,16,2,4224]{3,2,0,1:T(2,128)(2,1)}), bf16[2,16,2,4224]{3,2,0,1:T(2,128)(2,1)S(1)}, u32[]{:S(2)}, u32[]{:S(2)}) %all-to-all-start.2) | async-done | bytes 540704 | tf_op jit(solution)/shard_map/all_to_all | solution.py:101
  352.3 0.4 copy.69
  353.1 0.9 convolution_convert_fusion.8
  353.9 0.8 fusion.57
  (92 shorter events, 3.5 us)
Async XLA Ops:
  7.2 2.7 copy-start
  7.2 79.7 %all-gather.7.cloned.1.call-start = ((), (), s32[]{:S(2)}) async-start(), calls=%async_computation.7 | async-start | bytes 4792320 | tf_op jit(solution)/shard_map/expert_0/all_gather | solution.py:54
  8.4 1.3 copy-start.12
  31.1 112.1 %all-gather.9.cloned.1.call-start = ((), (), s32[]{:S(2)}) async-start(), calls=%async_computation.10 | async-start | bytes 4792320 | tf_op jit(solution)/shard_map/expert_1/all_gather | solution.py:54
  46.3 123.5 %all-gather.11.cloned.1.call-start = ((), (), s32[]{:S(2)}) async-start(), calls=%async_computation.13 | async-start | bytes 12779520 | tf_op jit(solution)/shard_map/expert_0/all_gather | solution.py:55
  86.8 83.9 %copy-start.2 = (bf16[2,96,4096]{2,1,0:T(8,128)(2,1)S(1)}, bf16[2,96,4096]{2,1,0:T(8,128)(2,1)}, u32[]{:S(2)}) copy-start(bf16[2,96,4096]{2,1,0:T(8,128)(2,1)} %param.11) | copy-start | bytes 4718596
  86.9 111.9 %all-gather.13.cloned.1.call-start = ((), (), s32[]{:S(2)}) async-start(), calls=%async_computation.14 | async-start | bytes 12779520 | tf_op jit(solution)/shard_map/expert_1/all_gather | solution.py:55
  143.2 31.3 %copy-start.3 = (bf16[2,96,4096]{2,1,0:T(8,128)(2,1)S(1)}, bf16[2,96,4096]{2,1,0:T(8,128)(2,1)}, u32[]{:S(2)}) copy-start(bf16[2,96,4096]{2,1,0:T(8,128)(2,1)} %param.12) | copy-start | bytes 4718596
  143.2 80.3 %reduce-scatter.5.cloned.1.call-start = ((), (), s32[]{:S(2)}) async-start(), calls=%async_computation.8 | async-start | bytes 6488064 | tf_op jit(solution)/shard_map/expert_0/reduce_scatter | solution.py:85
  170.8 7.5 %copy-start.10 = (bf16[16,32,8320]{2,1,0:T(8,128)(2,1)S(1)}, bf16[16,32,8320]{2,1,0:T(8,128)(2,1)}, u32[]{:S(2)}) copy-start(bf16[16,32,8320]{2,1,0:T(8,128)(2,1)} %all-gather.11.cloned.1.call-done) | copy-start | bytes 25559044
  174.6 5.9 %copy-start.16 = (f32[512,96]{0,1:T(8,128)}, f32[512,96]{0,1:T(8,128)S(1)}, u32[]{:S(2)}) copy-start(f32[512,96]{0,1:T(8,128)S(1)} %fusion.20) | copy-start | bytes 589828
  174.6 3.8 %copy-start.14 = (bf16[2,96,4096]{2,1,0:T(8,128)(2,1)S(1)}, bf16[2,96,4096]{2,1,0:T(8,128)(2,1)}, u32[]{:S(2)}) copy-start(bf16[2,96,4096]{2,1,0:T(8,128)(2,1)} %param.13) | copy-start | bytes 4718596
  178.3 2.1 copy-start.18
  180.4 2.7 copy-start.4
  194.5 48.0 %reduce-scatter.9.cloned.1.call-start = ((), (), s32[]{:S(2)}) async-start(), calls=%async_computation.11 | async-start | bytes 6488064 | tf_op jit(solution)/shard_map/expert_1/reduce_scatter | solution.py:85
  199.8 7.5 %copy-start.11 = (bf16[16,32,8320]{2,1,0:T(8,128)(2,1)S(1)}, bf16[16,32,8320]{2,1,0:T(8,128)(2,1)}, u32[]{:S(2)}) copy-start(bf16[16,32,8320]{2,1,0:T(8,128)(2,1)} %all-gather.13.cloned.1.call-done) | copy-start | bytes 25559044
  203.6 5.9 %copy-start.20 = (f32[512,96]{0,1:T(8,128)}, f32[512,96]{0,1:T(8,128)S(1)}, u32[]{:S(2)}) copy-start(f32[512,96]{0,1:T(8,128)S(1)} %fusion.14) | copy-start | bytes 589828
  203.6 3.8 %copy-start.15 = (bf16[2,96,4096]{2,1,0:T(8,128)(2,1)S(1)}, bf16[2,96,4096]{2,1,0:T(8,128)(2,1)}, u32[]{:S(2)}) copy-start(bf16[2,96,4096]{2,1,0:T(8,128)(2,1)} %param.13) | copy-start | bytes 4718596
  207.4 2.1 copy-start.22
  210.0 2.2 copy-start.7
  223.4 19.1 %copy-start.13 = (s32[32]{0:T(128)S(1)}, s32[32]{0:T(128)}, u32[]{:S(2)}) copy-start(s32[32]{0:T(128)} %copy-done.12) | copy-start | bytes 388
  223.4 19.2 %copy-start.9 = (bf16[512,96]{0,1:T(8,128)(2,1)S(1)}, bf16[512,96]{0,1:T(8,128)(2,1)}, u32[]{:S(2)}) copy-start(bf16[512,96]{0,1:T(8,128)(2,1)} %get-tuple-element.14) | copy-start | bytes 294916
  223.5 65.9 %reduce-scatter.7.cloned.1.call-start = ((), (), s32[]{:S(2)}) async-start(), calls=%async_computation.9 | async-start | bytes 2433024 | tf_op jit(solution)/shard_map/expert_0/reduce_scatter | solution.py:86
  224.2 21.5 %copy-start.8 = (bf16[512,96]{0,1:T(8,128)(2,1)S(1)}, bf16[512,96]{0,1:T(8,128)(2,1)}, u32[]{:S(2)}) copy-start(bf16[512,96]{0,1:T(8,128)(2,1)} %get-tuple-element.15) | copy-start | bytes 294916
  224.2 109.4 %reduce-scatter.11.cloned.1.call-start = ((), (), s32[]{:S(2)}) async-start(), calls=%async_computation.12 | async-start | bytes 2433024 | tf_op jit(solution)/shard_map/expert_1/reduce_scatter | solution.py:86
  242.6 6.1 %copy-start.6 = (bf16[512,96]{0,1:T(8,128)(2,1)S(1)}, bf16[512,96]{0,1:T(8,128)(2,1)}, u32[]{:S(2)}) copy-start(bf16[512,96]{0,1:T(8,128)(2,1)} %get-tuple-element.12) | copy-start | bytes 294916
  245.7 6.1 %copy-start.17 = (f32[512,96]{0,1:T(8,128)S(1)}, f32[512,96]{0,1:T(8,128)}, u32[]{:S(2)}) copy-start(f32[512,96]{0,1:T(8,128)} %copy-done.16) | copy-start | bytes 589828
  245.7 6.1 %copy-start.19 = (f32[512,96]{0,1:T(8,128)S(1)}, f32[512,96]{0,1:T(8,128)}, u32[]{:S(2)}) copy-start(f32[512,96]{0,1:T(8,128)} %copy-done.18) | copy-start | bytes 589828
  251.8 3.1 copy-start.21
  251.8 3.1 copy-start.23
  257.8 85.7 %copy-start.5 = (bf16[512,96]{0,1:T(8,128)(2,1)S(1)}, bf16[512,96]{0,1:T(8,128)(2,1)}, u32[]{:S(2)}) copy-start(bf16[512,96]{0,1:T(8,128)(2,1)} %copy-done.4) | copy-start | bytes 294916
  336.2 16.1 %all-to-all-start.2 = ((bf16[2,16,2,4224]{3,2,0,1:T(2,128)(2,1)}), bf16[2,16,2,4224]{3,2,0,1:T(2,128)(2,1)S(1)}, u32[]{:S(2)}, u32[]{:S(2)}) async-start(bf16[2,16,2,4224]{3,2,0,1:T(2,128)(2,1)} %pad_maximum_fusion.3), calls=%async_computation.6 | async-start | bytes 1081344 | tf_op jit(solution)/shard_map/all_to_all | solution.py:101
  343.5 11.2 %copy-start.1 = (bf16[16,4096]{1,0:T(8,128)(2,1)S(1)}, bf16[16,4096]{1,0:T(8,128)(2,1)}, u32[]{:S(2)}) copy-start(bf16[16,4096]{1,0:T(8,128)(2,1)} %param.8) | copy-start | bytes 393220
Sparse Core Ops, SparseCore 0:
  31.3 55.5 all-gather.6
  89.2 53.9 all-gather.8
  145.0 24.6 all-gather.10
  171.4 27.3 all-gather.12
  201.2 18.8 reduce-scatter.4
  223.6 18.8 reduce-scatter.8
  245.1 44.2 reduce-scatter.6
  291.9 41.6 reduce-scatter.10

commit v2 on v1

--- a/solution.py
+++ b/solution.py
@@ -1,10 +1,8 @@
 import jax
 import jax.numpy as jnp
 from jax import lax
-from jax.sharding import Mesh
 from jax.sharding import PartitionSpec as P
 
-CORES = 2
 PAD = 128
 
 
@@ -14,13 +12,12 @@
     chosen = routes.shape[1]
     local_experts = gate_weight.shape[0]
     groups = lax.axis_size("expert")
-    n_z = lax.axis_size("z")
-    n_core = lax.axis_size("core")
+    n_dp = lax.axis_size("dp")
     experts_all = local_experts * groups
     capacity = 2 * tok_rows * chosen // experts_all
     slot_count = experts_all * capacity
     block_rows = groups * capacity
-    gathered_rows = n_core * n_z * block_rows
+    gathered_rows = n_dp * block_rows
     width = 2 * model_width + PAD
     back_width = model_width + PAD
 
@@ -46,14 +43,16 @@
     payload = jnp.concatenate([x_slots, dy_slots, gate_cols], axis=1)
     payload = payload.reshape(local_experts, groups, capacity, width)
 
+    extra_rows = (
+        jnp.arange(back_width, dtype=jnp.int32)[None, :]
+        == model_width + jnp.arange(2, dtype=jnp.int32)[:, None]
+    ).astype(bf16)
     backs, ggw, guw, gdw = [], [], [], []
     for l in range(local_experts):
         with jax.named_scope(f"expert_{l}"):
             blk = lax.all_to_all(payload[l], "expert", split_axis=0, concat_axis=0, tiled=True)
             blk = blk.reshape(block_rows, width)
-            gz = lax.all_gather(blk, "z", axis=0)
-            gzc = lax.all_gather(gz, "core", axis=0)
-            rows = gzc.reshape(gathered_rows, width)
+            rows = lax.all_gather(blk, "dp", axis=0).reshape(gathered_rows, width)
             inputs = rows[:, :model_width]
             upstream = rows[:, model_width : 2 * model_width]
             weighting = rows[:, 2 * model_width].astype(f32)[:, None]
@@ -71,20 +70,16 @@
             ).astype(bf16)
             grad_up_pre = (scaled * activated).astype(bf16)
             weighted_hidden = (weighting * hidden).astype(bf16)
-            input_part = jnp.einsum("rh,hd->rd", grad_gate_pre, gw, preferred_element_type=f32)
-            input_part = input_part + jnp.einsum(
-                "rh,hd->rd", grad_up_pre, uw, preferred_element_type=f32
-            )
             hi = gate_part.astype(bf16)
             lo = (gate_part - hi.astype(f32)).astype(bf16)
-            tail = jnp.concatenate(
-                [hi[:, None], lo[:, None], jnp.zeros((gathered_rows, PAD - 2), bf16)], axis=1
-            )
-            back = jnp.concatenate([input_part.astype(bf16), tail], axis=1)
-            back = back.reshape(n_core, n_z, block_rows, back_width)
-            back = lax.psum_scatter(back, "core", scatter_dimension=0, tiled=True)
-            back = lax.psum_scatter(back, "z", scatter_dimension=1, tiled=True)
-            backs.append(back.reshape(groups, capacity, back_width))
+            lhs = jnp.concatenate([grad_gate_pre, grad_up_pre, hi[:, None], lo[:, None]], axis=1)
+            stacked = jnp.pad(jnp.concatenate([gw, uw], axis=0), ((0, 0), (0, PAD)))
+            rhs = jnp.concatenate([stacked, extra_rows], axis=0)
+            back = jnp.dot(lhs, rhs, preferred_element_type=f32).astype(bf16)
+            back = back.reshape(n_dp, block_rows, back_width)
+            back = lax.psum_scatter(back, "dp", scatter_dimension=0, tiled=True)
+            back = back.reshape(groups, capacity, back_width)
+            backs.append(lax.all_to_all(back, "expert", split_axis=0, concat_axis=0, tiled=True))
             ggw.append(
                 jnp.einsum("rh,rd->hd", grad_gate_pre, inputs, preferred_element_type=f32).astype(bf16)
             )
@@ -97,9 +92,7 @@
                 )
             )
 
-    back_all = jnp.stack(backs)
-    returned = lax.all_to_all(back_all, "expert", split_axis=1, concat_axis=1, tiled=True)
-    returned = returned.reshape(slot_count, back_width)
+    returned = jnp.stack(backs).reshape(slot_count, back_width)
     grad_tokens = lax.dot_general(
         token_map,
         returned[:, :model_width],
@@ -114,13 +107,11 @@
 
 
 def solution(mesh):
-    n_expert, n_dp = mesh.devices.shape
-    split = Mesh(mesh.devices.reshape(n_expert, n_dp // CORES, CORES), ("expert", "z", "core"))
-    rows = P(("expert", "z", "core"), None)
-    blocks = P("expert", ("z", "core"), None)
+    rows = P(("expert", "dp"), None)
+    blocks = P("expert", "dp", None)
     return jax.shard_map(
         per_device,
-        mesh=split,
+        mesh=mesh,
         in_specs=(rows, rows, rows, rows, blocks, blocks, blocks),
         out_specs=(rows, rows, blocks, blocks, blocks),
         check_vma=False,

time: 363 us -> 301 us (0.83)
  waiting for transfers between devices: 224 us -> 174 us
  local copies, waits for them, and re-layouts: 24.9 us -> 11.4 us
  starting transfers between devices: 7.75 us -> 14.9 us
  matrix products: 51.7 us -> 47.1 us
    all_gather x4 -> x2, waiting for transfers between devices: 127 us -> 82.2 us  [per_device(): rows = lax.all_gather(blk, 'dp', axis=0).reshape(gathered_rows, width)]
    concatenate x3 -> x0, local copies, waits for them, and re-layouts: 15.8 us -> none  [per_device(): back = jnp.concatenate([input_part.astype(bf16), tail], axis=1)]
    all_to_all x1 -> x2, starting transfers between devices: 7.25 us -> 14.5 us  [per_device(): lax.all_to_all(back, 'expert', split_axis=0, concat_axis=0, tiled=True)]
    reduce_scatter x4 -> x2, waiting for transfers between devices: 91 us -> 85.5 us  [per_device(): back = lax.psum_scatter(back, 'dp', scatter_dimension=0, tiled=True)]
    dot_general x4 -> x2, matrix products: 11.2 us -> 6.86 us  [per_device(): back = jnp.dot(lhs, rhs, preferred_element_type=f32).astype(bf16)]
    dot_general x2, matrix products: 7.52 us -> 3.59 us  [per_device(): gate_pre = jnp.einsum('rd,hd->rh', inputs, gw, preferred_element_type=f32)]
  transfers between devices with their start and end apart: 9 -> 6, of which waited for: 8 -> 5; matrix products, arithmetic and copies ran while one was open for 20% -> 19% of each run, Pallas kernels for 0% -> 0%
where the time goes in v2:
time: 301 us; the launch traced here: 300 us
  waiting for transfers between devices  174 us (58%)
  matrix products  47.1 us (16%)
  blocking collectives  31.6 us (10%)
  starting transfers between devices  14.9 us (5%)
  between operations  14.2 us (5%)
  local copies, waits for them, and re-layouts  11.4 us (4%)
  other arithmetic  7.28 us (2%)
    reduce_scatter x2, waiting for transfers between devices, per_device(): back = lax.psum_scatter(back, 'dp', scatter_dimension=0, tiled=True)  85.5 us
    all_gather x2, waiting for transfers between devices, per_device(): rows = lax.all_gather(blk, 'dp', axis=0).reshape(gathered_rows, width)  82.2 us
    all_to_all x2, blocking collectives, per_device(): lax.all_to_all(payload[l], 'expert', split_axis=0, concat_axis=0, tiled=T...  31.6 us
    all_to_all x2, starting transfers between devices, per_device(): lax.all_to_all(back, 'expert', split_axis=0, concat_axis=0, tiled=True)  14.5 us
    dot_general x2, matrix products, per_device(): up_pre = jnp.einsum('rd,hd->rh', inputs, uw, preferred_element_type=f32)  7.72 us
    dot_general x2, matrix products, per_device(): jnp.einsum('rd,hd->rh', upstream, dw, preferred_element_type=f32)  7.45 us
    dot_general x2, matrix products, per_device(): back = jnp.dot(lhs, rhs, preferred_element_type=f32).astype(bf16)  6.86 us
    dot_general x2, matrix products, per_device(): jnp.einsum('rh,rd->hd', grad_up_pre, inputs, preferred_element_type=f32)  6.18 us
  transfers between devices with their start and end apart: 6, of which 5 were waited for; matrix products, arithmetic and copies ran while one was open for 19% of the time, Pallas kernels for 0%

profile of v2, /device:TPU:8, one launch (start us, length us, event | category | flops | bytes accessed | tf_op | source)
XLA Modules:
  0.0 300.0 jit_solution(9476123266907842648)
XLA Ops:
  7.2 0.8 copy.44
  8.2 0.2 select_reduce_fusion
  8.5 0.8 copy.50
  9.8 0.3 convolution_convert_fusion.8
  10.1 1.2 convolution_convert_fusion.9
  11.4 0.8 concatenate.21
  12.2 0.2 squeeze.28
  12.5 17.7 %all_to_all.20 = bf16[16,2,8320]{2,1,0:T(2,128)(2,1)S(1)} all-to-all(bf16[16,2,8320]{2,1,0:T(2,128)(2,1)S(1)} %squeeze.28), channel_id=1, replica_groups=mesh['expert'=16,'dp'=16] {'expert'}, dimensions={0} | all-to-all | bytes 1064960 | tf_op jit(solution)/shard_map/expert_0/all_to_all | solution.py:53
  30.1 1.0 reshape.184
  31.2 0.2 squeeze.32
  31.4 14.0 %all_to_all.21 = bf16[16,2,8320]{2,1,0:T(2,128)(2,1)S(1)} all-to-all(bf16[16,2,8320]{2,1,0:T(2,128)(2,1)S(1)} %squeeze.32), channel_id=1, replica_groups=mesh['expert'=16,'dp'=16] {'expert'}, dimensions={0} | all-to-all | bytes 1064960 | tf_op jit(solution)/shard_map/expert_1/all_to_all | solution.py:53
  45.4 1.0 reshape.188
  46.5 1.5 slice_bitcast_fusion.2
  48.1 0.2 fusion.30
  48.4 39.5 %all-gather.3.cloned.1.call-done = bf16[16,32,8320]{2,1,0:T(8,128)(2,1)} async-done(((bf16[1,32,8320]{2,1,0:T(8,128)(2,1)}), bf16[16,32,8320]{2,1,0:T(8,128)(2,1)}) %all-gather.3.cloned.1.call-update) | async-done | bytes 8519696 | tf_op jit(solution)/shard_map/expert_0/all_gather | solution.py:55
  87.9 1.1 convert_reduce_fusion.1
  89.1 4.0 %fusion.26 = f32[512,96]{0,1:T(8,128)S(1)} fusion(bf16[512,8320]{1,0:T(8,128)(2,1)} %bitcast.82, bf16[2,96,4096]{2,1,0:T(8,128)(2,1)} %param.12), kind=kOutput, calls=%fused_computation.38 | convolution fusion | flops 402653184 | bytes 5177344 | tf_op jit(solution)/shard_map/expert_0/rd,hd->rh/dot_general | solution.py:61
  93.1 3.7 %fusion.10 = f32[512,96]{0,1:T(8,128)S(1)} fusion(bf16[512,8320]{1,0:T(8,128)(2,1)} %bitcast.83, bf16[2,96,4096]{2,1,0:T(8,128)(2,1)S(1)} %copy-done.7), kind=kOutput, calls=%fused_computation.21 | convolution fusion | flops 402653184 | bytes 5177344 | tf_op jit(solution)/shard_map/expert_0/rd,hd->rh/dot_general | solution.py:62
  96.9 2.1 multiply_convert_fusion.5
  99.0 3.5 %convolution_convert_fusion.1 = bf16[512,4224]{1,0:T(8,128)(2,1)} fusion(bf16[2,4224]{1,0:T(2,128)(2,1)S(1)} %compare_convert_fusion, bf16[192,4224]{1,0:T(8,128)(2,1)S(1)} %get-tuple-element.19, bf16[512,1]{0,1:T(2,128)(2,1)S(1)} %subtract_convert_fusion.1, bf16[512,1]{0,1:T(2,128)(2,1)S(1)} %convert_element_type.167, ...), kind=kOutput, calls=%fused_computation.1 | convolution fusion | flops 845358080 | bytes 6162944 | tf_op jit(solution)/shard_map/expert_0/dot_general | solution.py:78
  102.5 0.2 reduce-scatter.5.cloned.1.call-start
  102.7 42.7 %all-gather.5.cloned.1.call-done = bf16[16,32,8320]{2,1,0:T(8,128)(2,1)} async-done(((bf16[1,32,8320]{2,1,0:T(8,128)(2,1)}), bf16[16,32,8320]{2,1,0:T(8,128)(2,1)}) %all-gather.5.cloned.1.call-update) | async-done | bytes 8519696 | tf_op jit(solution)/shard_map/expert_1/all_gather | solution.py:55
  145.4 1.1 convert_reduce_fusion
  146.6 3.8 %fusion.20 = f32[512,96]{0,1:T(8,128)S(1)} fusion(bf16[512,8320]{1,0:T(8,128)(2,1)} %bitcast.75, bf16[2,96,4096]{2,1,0:T(8,128)(2,1)S(1)} %copy-done.2), kind=kOutput, calls=%fused_computation.32 | convolution fusion | flops 402653184 | bytes 5177344 | tf_op jit(solution)/shard_map/expert_1/rd,hd->rh/dot_general | solution.py:61
  150.3 3.7 %fusion.7 = f32[512,96]{0,1:T(8,128)S(1)} fusion(bf16[512,8320]{1,0:T(8,128)(2,1)} %bitcast.76, bf16[2,96,4096]{2,1,0:T(8,128)(2,1)S(1)} %copy-done.8), kind=kOutput, calls=%fused_computation.18 | convolution fusion | flops 402653184 | bytes 5177344 | tf_op jit(solution)/shard_map/expert_1/rd,hd->rh/dot_general | solution.py:62
  154.1 1.5 multiply_convert_fusion.3
  155.6 3.4 %convolution_convert_fusion = bf16[512,4224]{1,0:T(8,128)(2,1)} fusion(bf16[2,4224]{1,0:T(2,128)(2,1)S(1)} %compare_convert_fusion, bf16[192,4224]{1,0:T(8,128)(2,1)S(1)} %get-tuple-element.20, bf16[512,1]{0,1:T(2,128)(2,1)S(1)} %subtract_convert_fusion, bf16[512,1]{0,1:T(2,128)(2,1)S(1)} %convert_element_type.174, bf16[512,96]{0,1:T(8,128)(2,1)S(1)} %get-tuple-element.16, ...), kind=kOutput, calls=%fused_computation | convolution fusion | flops 845358080 | bytes 6162944 | tf_op jit(solution)/shard_map/expert_1/dot_general | solution.py:78
  159.2 0.8 copy-done.10
  159.9 3.0 fusion
  162.9 3.0 %fusion.2 = bf16[1,96,4096]{2,1,0:T(8,128)(2,1)S(1)} fusion(bf16[512,96]{0,1:T(8,128)(2,1)S(1)} %get-tuple-element.15, bf16[512,8320]{1,0:T(8,128)(2,1)} %bitcast.85), kind=kOutput, calls=%fused_computation.10 | convolution fusion | flops 403046400 | bytes 5079040 | tf_op jit(solution)/shard_map/expert_0/rh,rd->hd/dot_general | solution.py:87
  166.0 3.0 %fusion.1 = bf16[1,96,4096]{2,1,0:T(8,128)(2,1)S(1)} fusion(bf16[512,96]{0,1:T(8,128)(2,1)S(1)} %get-tuple-element.13, bf16[512,8320]{1,0:T(8,128)(2,1)} %bitcast.77), kind=kOutput, calls=%fused_computation.9 | convolution fusion | flops 403046400 | bytes 5079040 | tf_op jit(solution)/shard_map/expert_1/rh,rd->hd/dot_general | solution.py:84
  169.0 3.1 %fusion.3 = bf16[1,96,4096]{2,1,0:T(8,128)(2,1)S(1)} fusion(bf16[512,96]{0,1:T(8,128)(2,1)S(1)} %get-tuple-element.16, bf16[512,8320]{1,0:T(8,128)(2,1)} %bitcast.78), kind=kOutput, calls=%fused_computation.11 | convolution fusion | flops 403046400 | bytes 5079040 | tf_op jit(solution)/shard_map/expert_1/rh,rd->hd/dot_general | solution.py:87
  172.2 3.0 %fusion.4 = bf16[1,96,4096]{2,1,0:T(8,128)(2,1)S(1)} fusion(bf16[512,8320]{1,0:T(8,128)(2,1)} %bitcast.86, f32[512]{0:T(512)S(1)} %convert_reduce_fusion.1, f32[512,96]{0,1:T(8,128)S(1)} %copy-done.12, f32[512,96]{0,1:T(8,128)S(1)} %copy-done.13), kind=kOutput, calls=%fused_computation.12 | convolution fusion | flops 403390464 | bytes 5376000 | tf_op jit(solution)/shard_map/expert_0/rh,rd->hd/dot_general | solution.py:90
  175.2 1.9 pad_maximum_fusion.4
  177.1 33.0 %reduce-scatter.3.cloned.1.call-done = bf16[1,32,4224]{2,1,0:T(8,128)(2,1)} async-done(((bf16[16,32,4224]{2,1,0:T(8,128)(2,1)}), bf16[1,32,4224]{2,1,0:T(8,128)(2,1)}) %reduce-scatter.3.cloned.1.call-update) | async-done | bytes 270352 | tf_op jit(solution)/shard_map/expert_0/reduce_scatter | solution.py:80
  210.1 1.8 reshape.187
  211.9 7.3 %all-to-all-start.1 = ((bf16[16,2,4224]{2,1,0:T(2,128)(2,1)}), bf16[16,2,4224]{2,1,0:T(2,128)(2,1)S(1)}, u32[]{:S(2)}, u32[]{:S(2)}) async-start(bf16[16,2,4224]{2,1,0:T(2,128)(2,1)} %reshape.187), calls=%async_computation.2 | async-start | bytes 540672 | tf_op jit(solution)/shard_map/expert_0/all_to_all | solution.py:82
  219.1 3.0 fusion.5
  222.1 52.6 %reduce-scatter.5.cloned.1.call-done = bf16[1,32,4224]{2,1,0:T(8,128)(2,1)} async-done(((bf16[16,32,4224]{2,1,0:T(8,128)(2,1)}), bf16[1,32,4224]{2,1,0:T(8,128)(2,1)}) %reduce-scatter.5.cloned.1.call-update) | async-done | bytes 270352 | tf_op jit(solution)/shard_map/expert_1/reduce_scatter | solution.py:80
  274.7 1.8 reshape.191
  276.4 7.3 %all-to-all-start.3 = ((bf16[16,2,4224]{2,1,0:T(2,128)(2,1)}), bf16[16,2,4224]{2,1,0:T(2,128)(2,1)S(1)}, u32[]{:S(2)}, u32[]{:S(2)}) async-start(bf16[16,2,4224]{2,1,0:T(2,128)(2,1)} %reshape.191), calls=%async_computation.5 | async-start | bytes 540672 | tf_op jit(solution)/shard_map/expert_1/all_to_all | solution.py:82
  283.7 1.3 pad_maximum_fusion.6
  285.0 5.7 %all-to-all-done.3 = bf16[16,2,4224]{2,1,0:T(2,128)(2,1)S(1)} async-done(((bf16[16,2,4224]{2,1,0:T(2,128)(2,1)}), bf16[16,2,4224]{2,1,0:T(2,128)(2,1)S(1)}, u32[]{:S(2)}, u32[]{:S(2)}) %all-to-all-start.3) | async-done | bytes 270368 | tf_op jit(solution)/shard_map/expert_1/all_to_all | solution.py:82
  290.7 0.8 pad_maximum_fusion.7
  291.5 0.2 reshape.192
  291.7 0.8 convolution_convert_fusion.10
  292.5 0.2 add_reduce_fusion
  292.7 0.8 fusion.61
  (61 shorter events, 1.5 us)
Async XLA Ops:
  7.2 2.6 copy-start
  7.2 80.8 %all-gather.3.cloned.1.call-start = ((), (), s32[]{:S(2)}) async-start(), calls=%async_computation.6 | async-start | bytes 9052160 | tf_op jit(solution)/shard_map/expert_0/all_gather | solution.py:55
  31.1 114.3 %all-gather.5.cloned.1.call-start = ((), (), s32[]{:S(2)}) async-start(), calls=%async_computation.8 | async-start | bytes 9052160 | tf_op jit(solution)/shard_map/expert_1/all_gather | solution.py:55
  31.2 16.7 %copy-start.1 = (bf16[2,96,4096]{2,1,0:T(8,128)(2,1)S(1)}, bf16[2,96,4096]{2,1,0:T(8,128)(2,1)}, u32[]{:S(2)}) copy-start(bf16[2,96,4096]{2,1,0:T(8,128)(2,1)} %param.12) | copy-start | bytes 4718596
  46.4 163.7 %reduce-scatter.3.cloned.1.call-start = ((), (), s32[]{:S(2)}) async-start(), calls=%async_computation.7 | async-start | bytes 4595712 | tf_op jit(solution)/shard_map/expert_0/reduce_scatter | solution.py:80
  87.9 5.1 %copy-start.7 = (bf16[2,96,4096]{2,1,0:T(8,128)(2,1)S(1)}, bf16[2,96,4096]{2,1,0:T(8,128)(2,1)}, u32[]{:S(2)}) copy-start(bf16[2,96,4096]{2,1,0:T(8,128)(2,1)} %param.13) | copy-start | bytes 4718596
  89.1 7.8 %copy-start.6 = (bf16[16,32,8320]{2,1,0:T(8,128)(2,1)S(1)}, bf16[16,32,8320]{2,1,0:T(8,128)(2,1)}, u32[]{:S(2)}) copy-start(bf16[16,32,8320]{2,1,0:T(8,128)(2,1)} %all-gather.3.cloned.1.call-done) | copy-start | bytes 25559044
  93.1 3.8 %copy-start.11 = (f32[512,96]{0,1:T(8,128)}, f32[512,96]{0,1:T(8,128)S(1)}, u32[]{:S(2)}) copy-start(f32[512,96]{0,1:T(8,128)S(1)} %fusion.26) | copy-start | bytes 589828
  93.1 3.8 %copy-start.3 = (bf16[2,96,4096]{2,1,0:T(8,128)(2,1)S(1)}, bf16[2,96,4096]{2,1,0:T(8,128)(2,1)}, u32[]{:S(2)}) copy-start(bf16[2,96,4096]{2,1,0:T(8,128)(2,1)} %param.11) | copy-start | bytes 4718596
  98.9 3.5 %copy-start.9 = (bf16[512,96]{0,1:T(8,128)(2,1)}, bf16[512,96]{0,1:T(8,128)(2,1)S(1)}, u32[]{:S(2)}) copy-start(bf16[512,96]{0,1:T(8,128)(2,1)S(1)} %get-tuple-element.11) | copy-start | bytes 294916
  102.4 44.1 %copy-start.2 = (bf16[2,96,4096]{2,1,0:T(8,128)(2,1)S(1)}, bf16[2,96,4096]{2,1,0:T(8,128)(2,1)}, u32[]{:S(2)}) copy-start(bf16[2,96,4096]{2,1,0:T(8,128)(2,1)} %param.12) | copy-start | bytes 4718596
  102.5 172.2 %reduce-scatter.5.cloned.1.call-start = ((), (), s32[]{:S(2)}) async-start(), calls=%async_computation.9 | async-start | bytes 4595712 | tf_op jit(solution)/shard_map/expert_1/reduce_scatter | solution.py:80
  145.4 4.9 %copy-start.8 = (bf16[2,96,4096]{2,1,0:T(8,128)(2,1)S(1)}, bf16[2,96,4096]{2,1,0:T(8,128)(2,1)}, u32[]{:S(2)}) copy-start(bf16[2,96,4096]{2,1,0:T(8,128)(2,1)} %param.13) | copy-start | bytes 4718596
  146.5 7.6 %copy-start.5 = (bf16[16,32,8320]{2,1,0:T(8,128)(2,1)S(1)}, bf16[16,32,8320]{2,1,0:T(8,128)(2,1)}, u32[]{:S(2)}) copy-start(bf16[16,32,8320]{2,1,0:T(8,128)(2,1)} %all-gather.5.cloned.1.call-done) | copy-start | bytes 25559044
  150.3 3.8 %copy-start.14 = (f32[512,96]{0,1:T(8,128)}, f32[512,96]{0,1:T(8,128)S(1)}, u32[]{:S(2)}) copy-start(f32[512,96]{0,1:T(8,128)S(1)} %fusion.20) | copy-start | bytes 589828
  150.3 3.8 %copy-start.4 = (bf16[2,96,4096]{2,1,0:T(8,128)(2,1)S(1)}, bf16[2,96,4096]{2,1,0:T(8,128)(2,1)}, u32[]{:S(2)}) copy-start(bf16[2,96,4096]{2,1,0:T(8,128)(2,1)} %param.11) | copy-start | bytes 4718596
  159.0 0.9 copy-start.10
  169.0 3.2 %copy-start.12 = (f32[512,96]{0,1:T(8,128)S(1)}, f32[512,96]{0,1:T(8,128)}, u32[]{:S(2)}) copy-start(f32[512,96]{0,1:T(8,128)} %copy-done.11) | copy-start | bytes 589828
  169.0 3.2 %copy-start.13 = (f32[512,96]{0,1:T(8,128)S(1)}, f32[512,96]{0,1:T(8,128)}, u32[]{:S(2)}) copy-start(f32[512,96]{0,1:T(8,128)} %get-tuple-element.18) | copy-start | bytes 589828
  175.2 43.9 %copy-start.15 = (f32[512,96]{0,1:T(8,128)S(1)}, f32[512,96]{0,1:T(8,128)}, u32[]{:S(2)}) copy-start(f32[512,96]{0,1:T(8,128)} %copy-done.14) | copy-start | bytes 589828
  211.9 64.6 %all-to-all-start.1 = ((bf16[16,2,4224]{2,1,0:T(2,128)(2,1)}), bf16[16,2,4224]{2,1,0:T(2,128)(2,1)S(1)}, u32[]{:S(2)}, u32[]{:S(2)}) async-start(bf16[16,2,4224]{2,1,0:T(2,128)(2,1)} %reshape.187), calls=%async_computation.2 | async-start | bytes 540672 | tf_op jit(solution)/shard_map/expert_0/all_to_all | solution.py:82
  276.4 14.3 %all-to-all-start.3 = ((bf16[16,2,4224]{2,1,0:T(2,128)(2,1)}), bf16[16,2,4224]{2,1,0:T(2,128)(2,1)S(1)}, u32[]{:S(2)}, u32[]{:S(2)}) async-start(bf16[16,2,4224]{2,1,0:T(2,128)(2,1)} %reshape.191), calls=%async_computation.5 | async-start | bytes 540672 | tf_op jit(solution)/shard_map/expert_1/all_to_all | solution.py:82
Sparse Core Ops, SparseCore 0:
  31.3 56.6 all-gather.2
  90.3 55.0 all-gather.4
  148.0 62.1 reduce-scatter.2
  212.5 62.1 reduce-scatter.4

commit v3 on v2

--- a/solution.py
+++ b/solution.py
@@ -76,10 +76,7 @@
             stacked = jnp.pad(jnp.concatenate([gw, uw], axis=0), ((0, 0), (0, PAD)))
             rhs = jnp.concatenate([stacked, extra_rows], axis=0)
             back = jnp.dot(lhs, rhs, preferred_element_type=f32).astype(bf16)
-            back = back.reshape(n_dp, block_rows, back_width)
-            back = lax.psum_scatter(back, "dp", scatter_dimension=0, tiled=True)
-            back = back.reshape(groups, capacity, back_width)
-            backs.append(lax.all_to_all(back, "expert", split_axis=0, concat_axis=0, tiled=True))
+            backs.append(back.reshape(n_dp, block_rows, back_width))
             ggw.append(
                 jnp.einsum("rh,rd->hd", grad_gate_pre, inputs, preferred_element_type=f32).astype(bf16)
             )
@@ -92,7 +89,10 @@
                 )
             )
 
-    returned = jnp.stack(backs).reshape(slot_count, back_width)
+    back = lax.psum_scatter(jnp.concatenate(backs, axis=1), "dp", scatter_dimension=0, tiled=True)
+    back = back.reshape(local_experts, groups, capacity, back_width)
+    returned = lax.all_to_all(back, "expert", split_axis=1, concat_axis=1, tiled=True)
+    returned = returned.reshape(slot_count, back_width)
     grad_tokens = lax.dot_general(
         token_map,
         returned[:, :model_width],

time: 301 us -> 273 us (0.907)
  waiting for transfers between devices: 174 us -> 148 us
  starting transfers between devices: 14.9 us -> 7.56 us
  other arithmetic: 7.28 us -> 14.5 us
    reduce_scatter x2 -> x1, waiting for transfers between devices: 85.5 us -> 51.7 us  [per_device(): lax.psum_scatter(jnp.concatenate(backs, axis=1), 'dp', scatter_dimension=...]
    all_gather x2, waiting for transfers between devices: 82.2 us -> 91.3 us  [per_device(): rows = lax.all_gather(blk, 'dp', axis=0).reshape(gathered_rows, width)]
    concatenate x0 -> x1, other arithmetic: none -> 7.8 us  [per_device(): jnp.concatenate(backs, axis=1)]
    all_to_all x2 -> x1, starting transfers between devices: 14.5 us -> 7.26 us  [per_device(): lax.all_to_all(back, 'expert', split_axis=1, concat_axis=1, tiled=True)]
  transfers between devices with their start and end apart: 6 -> 4, of which waited for: 5 -> 4; matrix products, arithmetic and copies ran while one was open for 19% -> 11% of each run, Pallas kernels for 0% -> 0%
where the time goes in v3:
time: 273 us
  waiting for transfers between devices  148 us (54%)
  matrix products  46.5 us (17%)
  blocking collectives  31.6 us (12%)
  other arithmetic  14.5 us (5%)
  between operations  14.1 us (5%)
  local copies, waits for them, and re-layouts  10.9 us (4%)
  starting transfers between devices  7.56 us (3%)
    all_gather x2, waiting for transfers between devices, per_device(): rows = lax.all_gather(blk, 'dp', axis=0).reshape(gathered_rows, width)  91.3 us
    reduce_scatter x1, waiting for transfers between devices, per_device(): lax.psum_scatter(jnp.concatenate(backs, axis=1), 'dp', scatter_dimension=...  51.7 us
    all_to_all x2, blocking collectives, per_device(): lax.all_to_all(payload[l], 'expert', split_axis=0, concat_axis=0, tiled=T...  31.6 us
    dot_general x2, matrix products, per_device(): up_pre = jnp.einsum('rd,hd->rh', inputs, uw, preferred_element_type=f32)  8.46 us
    concatenate x1, other arithmetic, per_device(): jnp.concatenate(backs, axis=1)  7.8 us
    all_to_all x1, starting transfers between devices, per_device(): lax.all_to_all(back, 'expert', split_axis=1, concat_axis=1, tiled=True)  7.26 us
    dot_general x2, matrix products, per_device(): back = jnp.dot(lhs, rhs, preferred_element_type=f32).astype(bf16)  6.85 us
    dot_general x2, matrix products, per_device(): jnp.einsum('rh,rd->hd', weighted_hidden, upstream, preferred_element_type...  6.2 us
  transfers between devices with their start and end apart: 4, of which 4 were waited for; matrix products, arithmetic and copies ran while one was open for 11% of the time, Pallas kernels for 0%

profile of v3, /device:TPU:8, one launch (start us, length us, event | category | flops | bytes accessed | tf_op | source)
XLA Modules:
  0.0 272.8 jit_solution(8301096907189134309)
XLA Ops:
  7.2 0.8 copy.53
  8.2 0.2 select_reduce_fusion
  8.5 0.8 copy.59
  9.8 0.3 convolution_convert_fusion.8
  10.1 1.2 convolution_convert_fusion.9
  11.4 0.8 concatenate.24
  12.2 0.2 squeeze.28
  12.5 17.7 %all_to_all.15 = bf16[16,2,8320]{2,1,0:T(2,128)(2,1)S(1)} all-to-all(bf16[16,2,8320]{2,1,0:T(2,128)(2,1)S(1)} %squeeze.28), channel_id=1, replica_groups=mesh['expert'=16,'dp'=16] {'expert'}, dimensions={0} | all-to-all | bytes 1064960 | tf_op jit(solution)/shard_map/expert_0/all_to_all | solution.py:53
  30.1 1.0 reshape.181
  31.2 0.2 squeeze.32
  31.4 14.0 %all_to_all.16 = bf16[16,2,8320]{2,1,0:T(2,128)(2,1)S(1)} all-to-all(bf16[16,2,8320]{2,1,0:T(2,128)(2,1)S(1)} %squeeze.32), channel_id=1, replica_groups=mesh['expert'=16,'dp'=16] {'expert'}, dimensions={0} | all-to-all | bytes 1064960 | tf_op jit(solution)/shard_map/expert_1/all_to_all | solution.py:53
  45.4 1.0 reshape.184
  46.4 0.2 reduce-scatter.2.cloned.1.call-start
  46.6 1.5 slice_bitcast_fusion.2
  48.2 0.2 fusion.30
  48.6 39.4 %all-gather.3.cloned.1.call-done = bf16[16,32,8320]{2,1,0:T(8,128)(2,1)} async-done(((bf16[1,32,8320]{2,1,0:T(8,128)(2,1)}), bf16[16,32,8320]{2,1,0:T(8,128)(2,1)}) %all-gather.3.cloned.1.call-update) | async-done | bytes 8519696 | tf_op jit(solution)/shard_map/expert_0/all_gather | solution.py:55
  87.9 1.0 convert_reduce_fusion.1
  89.0 4.5 %fusion.26 = f32[512,96]{0,1:T(8,128)} fusion(bf16[512,8320]{1,0:T(8,128)(2,1)} %bitcast.78, bf16[2,96,4096]{2,1,0:T(8,128)(2,1)} %param.12), kind=kOutput, calls=%fused_computation.39 | convolution fusion | flops 402653184 | bytes 5177344 | tf_op jit(solution)/shard_map/expert_0/rd,hd->rh/dot_general | solution.py:61
  93.5 51.9 %all-gather.5.cloned.1.call-done = bf16[16,32,8320]{2,1,0:T(8,128)(2,1)} async-done(((bf16[1,32,8320]{2,1,0:T(8,128)(2,1)}), bf16[16,32,8320]{2,1,0:T(8,128)(2,1)}) %all-gather.5.cloned.1.call-update) | async-done | bytes 8519696 | tf_op jit(solution)/shard_map/expert_1/all_gather | solution.py:55
  145.4 4.0 %fusion.20 = f32[512,96]{0,1:T(8,128)S(1)} fusion(bf16[512,8320]{1,0:T(8,128)(2,1)} %bitcast.70, bf16[2,96,4096]{2,1,0:T(8,128)(2,1)} %param.12), kind=kOutput, calls=%fused_computation.33 | convolution fusion | flops 402653184 | bytes 5177344 | tf_op jit(solution)/shard_map/expert_1/rd,hd->rh/dot_general | solution.py:61
  149.4 1.5 convert_reduce_fusion
  150.9 4.0 %fusion.10 = f32[512,96]{0,1:T(8,128)S(1)} fusion(bf16[512,8320]{1,0:T(8,128)(2,1)} %bitcast.79, bf16[2,96,4096]{2,1,0:T(8,128)(2,1)} %param.13), kind=kOutput, calls=%fused_computation.22 | convolution fusion | flops 402653184 | bytes 5177344 | tf_op jit(solution)/shard_map/expert_0/rd,hd->rh/dot_general | solution.py:62
  154.9 1.4 fusion.7
  156.3 0.2 copy-done.2
  156.5 2.1 multiply_convert_fusion.5
  158.6 2.1 multiply_convert_fusion.3
  160.7 3.4 %convolution_convert_fusion.1 = bf16[512,4224]{1,0:T(8,128)(2,1)} fusion(bf16[2,4224]{1,0:T(2,128)(2,1)S(1)} %compare_convert_fusion, bf16[192,4224]{1,0:T(8,128)(2,1)S(1)} %get-tuple-element.19, bf16[512,1]{0,1:T(2,128)(2,1)S(1)} %subtract_convert_fusion.1, bf16[512,1]{0,1:T(2,128)(2,1)S(1)} %convert_element_type.167, ...), kind=kOutput, calls=%fused_computation.2 | convolution fusion | flops 845358080 | bytes 6162944 | tf_op jit(solution)/shard_map/expert_0/dot_general | solution.py:78
  164.1 3.5 %convolution_convert_fusion = bf16[512,4224]{1,0:T(8,128)(2,1)} fusion(bf16[2,4224]{1,0:T(2,128)(2,1)S(1)} %compare_convert_fusion, bf16[192,4224]{1,0:T(8,128)(2,1)S(1)} %get-tuple-element.20, bf16[512,1]{0,1:T(2,128)(2,1)S(1)} %subtract_convert_fusion, bf16[512,1]{0,1:T(2,128)(2,1)S(1)} %convert_element_type.174, ...), kind=kOutput, calls=%fused_computation.1 | convolution fusion | flops 845358080 | bytes 6162944 | tf_op jit(solution)/shard_map/expert_1/dot_general | solution.py:78
  167.6 7.8 %pad_maximum_fusion = bf16[16,64,4224]{2,1,0:T(8,128)(2,1)} fusion(bf16[16,32,4224]{2,1,0:T(8,128)(2,1)} %bitcast.65, bf16[16,32,4224]{2,1,0:T(8,128)(2,1)} %bitcast.64), kind=kLoop, calls=%fused_computation | loop fusion | flops 17301504 | bytes 17301504 | tf_op jit(solution)/shard_map/concatenate | solution.py:92
  175.5 0.8 copy-done.7
  176.3 3.0 %fusion = bf16[1,96,4096]{2,1,0:T(8,128)(2,1)S(1)} fusion(bf16[512,96]{0,1:T(8,128)(2,1)S(1)} %copy-done.7, bf16[512,8320]{1,0:T(8,128)(2,1)} %bitcast.80), kind=kOutput, calls=%fused_computation.9 | convolution fusion | flops 403046400 | bytes 5079040 | tf_op jit(solution)/shard_map/expert_0/rh,rd->hd/dot_general | solution.py:81
  179.3 3.0 %fusion.2 = bf16[1,96,4096]{2,1,0:T(8,128)(2,1)S(1)} fusion(bf16[512,96]{0,1:T(8,128)(2,1)S(1)} %get-tuple-element.15, bf16[512,8320]{1,0:T(8,128)(2,1)} %bitcast.81), kind=kOutput, calls=%fused_computation.11 | convolution fusion | flops 403046400 | bytes 5079040 | tf_op jit(solution)/shard_map/expert_0/rh,rd->hd/dot_general | solution.py:84
  182.4 3.0 %fusion.1 = bf16[1,96,4096]{2,1,0:T(8,128)(2,1)S(1)} fusion(bf16[512,96]{0,1:T(8,128)(2,1)S(1)} %copy-done.11, bf16[512,8320]{1,0:T(8,128)(2,1)} %bitcast.72), kind=kOutput, calls=%fused_computation.10 | convolution fusion | flops 403046400 | bytes 5079040 | tf_op jit(solution)/shard_map/expert_1/rh,rd->hd/dot_general | solution.py:81
  185.4 3.1 %fusion.3 = bf16[1,96,4096]{2,1,0:T(8,128)(2,1)S(1)} fusion(bf16[512,96]{0,1:T(8,128)(2,1)S(1)} %copy-done.9, bf16[512,8320]{1,0:T(8,128)(2,1)} %bitcast.73), kind=kOutput, calls=%fused_computation.12 | convolution fusion | flops 403046400 | bytes 5079040 | tf_op jit(solution)/shard_map/expert_1/rh,rd->hd/dot_general | solution.py:84
  188.5 3.2 %fusion.4 = bf16[1,96,4096]{2,1,0:T(8,128)(2,1)S(1)} fusion(bf16[512,8320]{1,0:T(8,128)(2,1)} %bitcast.82, f32[512]{0:T(512)S(1)} %convert_reduce_fusion.1, f32[512,96]{0,1:T(8,128)S(1)} %copy-done.16, f32[512,96]{0,1:T(8,128)S(1)} %copy-done.17), kind=kOutput, calls=%fused_computation.13 | convolution fusion | flops 403390464 | bytes 5376000 | tf_op jit(solution)/shard_map/expert_0/rh,rd->hd/dot_general | solution.py:87
  191.8 1.9 pad_maximum_fusion.5
  193.7 51.7 %reduce-scatter.2.cloned.1.call-done = bf16[1,64,4224]{2,1,0:T(8,128)(2,1)} async-done(((bf16[16,64,4224]{2,1,0:T(8,128)(2,1)}), bf16[1,64,4224]{2,1,0:T(8,128)(2,1)}) %reduce-scatter.2.cloned.1.call-update) | async-done | bytes 540688 | tf_op jit(solution)/shard_map/reduce_scatter | solution.py:92
  245.4 1.2 reshape.187
  246.6 1.2 copy.61
  247.8 7.3 %all-to-all-start.2 = ((bf16[2,16,2,4224]{3,2,0,1:T(2,128)(2,1)}), bf16[2,16,2,4224]{3,2,0,1:T(2,128)(2,1)S(1)}, u32[]{:S(2)}, u32[]{:S(2)}) async-start(bf16[2,16,2,4224]{3,2,0,1:T(2,128)(2,1)} %copy.61), calls=%async_computation.3 | async-start | bytes 1081344 | tf_op jit(solution)/shard_map/all_to_all | solution.py:94
  255.1 3.0 %fusion.5 = bf16[1,96,4096]{2,1,0:T(8,128)(2,1)S(1)} fusion(bf16[512,8320]{1,0:T(8,128)(2,1)} %bitcast.74, f32[512]{0:T(512)S(1)} %convert_reduce_fusion, f32[512,96]{0,1:T(8,128)S(1)} %copy-done.13, f32[512,96]{0,1:T(8,128)S(1)} %copy-done.14), kind=kOutput, calls=%fused_computation.14 | convolution fusion | flops 403390464 | bytes 5376000 | tf_op jit(solution)/shard_map/expert_1/rh,rd->hd/dot_general | solution.py:87
  258.1 1.3 pad_maximum_fusion.7
  259.4 4.5 %all-to-all-done.2 = bf16[2,16,2,4224]{3,2,0,1:T(2,128)(2,1)S(1)} async-done(((bf16[2,16,2,4224]{3,2,0,1:T(2,128)(2,1)}), bf16[2,16,2,4224]{3,2,0,1:T(2,128)(2,1)S(1)}, u32[]{:S(2)}, u32[]{:S(2)}) %all-to-all-start.2) | async-done | bytes 540704 | tf_op jit(solution)/shard_map/all_to_all | solution.py:94
  263.9 0.4 copy.62
  264.3 0.2 reshape.188
  264.5 0.8 convolution_convert_fusion.10
  265.3 0.2 add_reduce_fusion
  265.5 0.8 fusion.61
  (61 shorter events, 1.4 us)
Async XLA Ops:
  7.2 2.6 copy-start
  7.2 80.8 %all-gather.3.cloned.1.call-start = ((), (), s32[]{:S(2)}) async-start(), calls=%async_computation.4 | async-start | bytes 9052160 | tf_op jit(solution)/shard_map/expert_0/all_gather | solution.py:55
  31.1 114.3 %all-gather.5.cloned.1.call-start = ((), (), s32[]{:S(2)}) async-start(), calls=%async_computation.5 | async-start | bytes 9052160 | tf_op jit(solution)/shard_map/expert_1/all_gather | solution.py:55
  31.2 16.9 %copy-start.1 = (bf16[2,96,4096]{2,1,0:T(8,128)(2,1)S(1)}, bf16[2,96,4096]{2,1,0:T(8,128)(2,1)}, u32[]{:S(2)}) copy-start(bf16[2,96,4096]{2,1,0:T(8,128)(2,1)} %param.12) | copy-start | bytes 4718596
  46.4 199.0 %reduce-scatter.2.cloned.1.call-start = ((), (), s32[]{:S(2)}) async-start(), calls=%async_computation.6 | async-start | bytes 9191424 | tf_op jit(solution)/shard_map/reduce_scatter | solution.py:92
  145.4 9.4 %copy-start.3 = (bf16[16,32,8320]{2,1,0:T(8,128)(2,1)S(1)}, bf16[16,32,8320]{2,1,0:T(8,128)(2,1)}, u32[]{:S(2)}) copy-start(bf16[16,32,8320]{2,1,0:T(8,128)(2,1)} %all-gather.5.cloned.1.call-done) | copy-start | bytes 25559044
  145.4 9.5 %copy-start.5 = (bf16[2,96,4096]{2,1,0:T(8,128)(2,1)S(1)}, bf16[2,96,4096]{2,1,0:T(8,128)(2,1)}, u32[]{:S(2)}) copy-start(bf16[2,96,4096]{2,1,0:T(8,128)(2,1)} %param.13) | copy-start | bytes 4718596
  149.4 9.2 %copy-start.12 = (f32[512,96]{0,1:T(8,128)}, f32[512,96]{0,1:T(8,128)S(1)}, u32[]{:S(2)}) copy-start(f32[512,96]{0,1:T(8,128)S(1)} %fusion.20) | copy-start | bytes 589828
  150.8 5.4 %copy-start.4 = (bf16[16,32,8320]{2,1,0:T(8,128)(2,1)S(1)}, bf16[16,32,8320]{2,1,0:T(8,128)(2,1)}, u32[]{:S(2)}) copy-start(bf16[16,32,8320]{2,1,0:T(8,128)(2,1)} %all-gather.3.cloned.1.call-done) | copy-start | bytes 25559044
  154.8 1.6 copy-start.2
  154.9 1.6 copy-start.15
  158.6 2.1 copy-start.6
  160.7 6.9 %copy-start.8 = (bf16[512,96]{0,1:T(8,128)(2,1)}, bf16[512,96]{0,1:T(8,128)(2,1)S(1)}, u32[]{:S(2)}) copy-start(bf16[512,96]{0,1:T(8,128)(2,1)S(1)} %get-tuple-element.16) | copy-start | bytes 294916
  160.7 6.9 %copy-start.10 = (bf16[512,96]{0,1:T(8,128)(2,1)}, bf16[512,96]{0,1:T(8,128)(2,1)S(1)}, u32[]{:S(2)}) copy-start(bf16[512,96]{0,1:T(8,128)(2,1)S(1)} %get-tuple-element.13) | copy-start | bytes 294916
  175.4 0.9 copy-start.7
  179.3 3.1 %copy-start.11 = (bf16[512,96]{0,1:T(8,128)(2,1)S(1)}, bf16[512,96]{0,1:T(8,128)(2,1)}, u32[]{:S(2)}) copy-start(bf16[512,96]{0,1:T(8,128)(2,1)} %copy-done.10) | copy-start | bytes 294916
  182.3 3.0 %copy-start.9 = (bf16[512,96]{0,1:T(8,128)(2,1)S(1)}, bf16[512,96]{0,1:T(8,128)(2,1)}, u32[]{:S(2)}) copy-start(bf16[512,96]{0,1:T(8,128)(2,1)} %copy-done.8) | copy-start | bytes 294916
  185.4 3.1 %copy-start.16 = (f32[512,96]{0,1:T(8,128)S(1)}, f32[512,96]{0,1:T(8,128)}, u32[]{:S(2)}) copy-start(f32[512,96]{0,1:T(8,128)} %fusion.26) | copy-start | bytes 589828
  185.4 3.1 %copy-start.17 = (f32[512,96]{0,1:T(8,128)S(1)}, f32[512,96]{0,1:T(8,128)}, u32[]{:S(2)}) copy-start(f32[512,96]{0,1:T(8,128)} %get-tuple-element.18) | copy-start | bytes 589828
  191.7 63.3 %copy-start.13 = (f32[512,96]{0,1:T(8,128)S(1)}, f32[512,96]{0,1:T(8,128)}, u32[]{:S(2)}) copy-start(f32[512,96]{0,1:T(8,128)} %copy-done.12) | copy-start | bytes 589828
  191.7 63.3 %copy-start.14 = (f32[512,96]{0,1:T(8,128)S(1)}, f32[512,96]{0,1:T(8,128)}, u32[]{:S(2)}) copy-start(f32[512,96]{0,1:T(8,128)} %get-tuple-element.17) | copy-start | bytes 589828
  247.8 16.1 %all-to-all-start.2 = ((bf16[2,16,2,4224]{3,2,0,1:T(2,128)(2,1)}), bf16[2,16,2,4224]{3,2,0,1:T(2,128)(2,1)S(1)}, u32[]{:S(2)}, u32[]{:S(2)}) async-start(bf16[2,16,2,4224]{3,2,0,1:T(2,128)(2,1)} %copy.61), calls=%async_computation.3 | async-start | bytes 1081344 | tf_op jit(solution)/shard_map/all_to_all | solution.py:94
Sparse Core Ops, SparseCore 0:
  31.3 56.6 all-gather.2
  90.3 55.0 all-gather.4
  175.5 69.8 reduce-scatter.1

commit v4 on v3

--- a/solution.py
+++ b/solution.py
@@ -2,6 +2,7 @@
 import jax.numpy as jnp
 from jax import lax
 from jax.sharding import PartitionSpec as P
+
 
 PAD = 128
 
@@ -49,45 +50,46 @@
     ).astype(bf16)
     backs, ggw, guw, gdw = [], [], [], []
     for l in range(local_experts):
-        with jax.named_scope(f"expert_{l}"):
-            blk = lax.all_to_all(payload[l], "expert", split_axis=0, concat_axis=0, tiled=True)
-            blk = blk.reshape(block_rows, width)
-            rows = lax.all_gather(blk, "dp", axis=0).reshape(gathered_rows, width)
-            inputs = rows[:, :model_width]
-            upstream = rows[:, model_width : 2 * model_width]
-            weighting = rows[:, 2 * model_width].astype(f32)[:, None]
-            gw, uw, dw = gate_weight[l], up_weight[l], down_weight[l]
-            gate_pre = jnp.einsum("rd,hd->rh", inputs, gw, preferred_element_type=f32)
-            up_pre = jnp.einsum("rd,hd->rh", inputs, uw, preferred_element_type=f32)
-            back_hidden = jnp.einsum("rd,hd->rh", upstream, dw, preferred_element_type=f32)
-            sigmoid_gate = jax.nn.sigmoid(gate_pre)
-            activated = gate_pre * sigmoid_gate
-            hidden = activated * up_pre
-            gate_part = jnp.sum(back_hidden * hidden, axis=1)
-            scaled = weighting * back_hidden
-            grad_gate_pre = (
-                scaled * up_pre * sigmoid_gate * (1.0 + gate_pre * (1.0 - sigmoid_gate))
-            ).astype(bf16)
-            grad_up_pre = (scaled * activated).astype(bf16)
-            weighted_hidden = (weighting * hidden).astype(bf16)
-            hi = gate_part.astype(bf16)
-            lo = (gate_part - hi.astype(f32)).astype(bf16)
-            lhs = jnp.concatenate([grad_gate_pre, grad_up_pre, hi[:, None], lo[:, None]], axis=1)
-            stacked = jnp.pad(jnp.concatenate([gw, uw], axis=0), ((0, 0), (0, PAD)))
-            rhs = jnp.concatenate([stacked, extra_rows], axis=0)
-            back = jnp.dot(lhs, rhs, preferred_element_type=f32).astype(bf16)
-            backs.append(back.reshape(n_dp, block_rows, back_width))
-            ggw.append(
-                jnp.einsum("rh,rd->hd", grad_gate_pre, inputs, preferred_element_type=f32).astype(bf16)
+        blk = lax.all_to_all(payload[l], "expert", split_axis=0, concat_axis=0, tiled=True)
+        blk = blk.reshape(block_rows, width)
+        rows = lax.all_gather(blk, "dp", axis=0).reshape(gathered_rows, width)
+        inputs = rows[:, :model_width]
+        upstream = rows[:, model_width : 2 * model_width]
+        weighting = rows[:, 2 * model_width].astype(f32)[:, None]
+        gw, uw, dw = gate_weight[l], up_weight[l], down_weight[l]
+        gate_pre = jnp.einsum("rd,hd->rh", inputs, gw, preferred_element_type=f32)
+        up_pre = jnp.einsum("rd,hd->rh", inputs, uw, preferred_element_type=f32)
+        back_hidden = jnp.einsum("rd,hd->rh", upstream, dw, preferred_element_type=f32)
+        sigmoid_gate = jax.nn.sigmoid(gate_pre)
+        activated = gate_pre * sigmoid_gate
+        hidden = activated * up_pre
+        gate_part = jnp.sum(back_hidden * hidden, axis=1)
+        scaled = weighting * back_hidden
+        grad_gate_pre = (
+            scaled * up_pre * sigmoid_gate * (1.0 + gate_pre * (1.0 - sigmoid_gate))
+        ).astype(bf16)
+        grad_up_pre = (scaled * activated).astype(bf16)
+        weighted_hidden = (weighting * hidden).astype(bf16)
+        hi = gate_part.astype(bf16)
+        lo = (gate_part - hi.astype(f32)).astype(bf16)
+        lhs = jnp.concatenate(
+            [grad_gate_pre, grad_up_pre, hi[:, None], lo[:, None]], axis=1
+        )
+        stacked = jnp.pad(jnp.concatenate([gw, uw], axis=0), ((0, 0), (0, PAD)))
+        rhs = jnp.concatenate([stacked, extra_rows], axis=0)
+        back = jnp.dot(lhs, rhs, preferred_element_type=f32).astype(bf16)
+        backs.append(back.reshape(n_dp, block_rows, back_width))
+        ggw.append(
+            jnp.einsum("rh,rd->hd", grad_gate_pre, inputs, preferred_element_type=f32).astype(bf16)
+        )
+        guw.append(
+            jnp.einsum("rh,rd->hd", grad_up_pre, inputs, preferred_element_type=f32).astype(bf16)
+        )
+        gdw.append(
+            jnp.einsum("rh,rd->hd", weighted_hidden, upstream, preferred_element_type=f32).astype(
+                bf16
             )
-            guw.append(
-                jnp.einsum("rh,rd->hd", grad_up_pre, inputs, preferred_element_type=f32).astype(bf16)
-            )
-            gdw.append(
-                jnp.einsum("rh,rd->hd", weighted_hidden, upstream, preferred_element_type=f32).astype(
-                    bf16
-                )
-            )
+        )
 
     back = lax.psum_scatter(jnp.concatenate(backs, axis=1), "dp", scatter_dimension=0, tiled=True)
     back = back.reshape(local_experts, groups, capacity, back_width)

time: 273 us -> 273 us (level)
  no operation moved by 1% of the time
where the time goes in v4:
time: 273 us
  waiting for transfers between devices  148 us (54%)
  matrix products  46.5 us (17%)
  blocking collectives  31.6 us (12%)
  other arithmetic  14.5 us (5%)
  between operations  14.1 us (5%)
  local copies, waits for them, and re-layouts  10.9 us (4%)
  starting transfers between devices  7.56 us (3%)
    all_gather x2, waiting for transfers between devices, per_device(): rows = lax.all_gather(blk, 'dp', axis=0).reshape(gathered_rows, width)  91.3 us
    reduce_scatter x1, waiting for transfers between devices, per_device(): lax.psum_scatter(jnp.concatenate(backs, axis=1), 'dp', scatter_dimension=...  51.7 us
    all_to_all x2, blocking collectives, per_device(): lax.all_to_all(payload[l], 'expert', split_axis=0, concat_axis=0, tiled=T...  31.6 us
    dot_general x2, matrix products, per_device(): up_pre = jnp.einsum('rd,hd->rh', inputs, uw, preferred_element_type=f32)  8.46 us
    concatenate x1, other arithmetic, per_device(): jnp.concatenate(backs, axis=1)  7.8 us
    all_to_all x1, starting transfers between devices, per_device(): lax.all_to_all(back, 'expert', split_axis=1, concat_axis=1, tiled=True)  7.26 us
    dot_general x2, matrix products, per_device(): back = jnp.dot(lhs, rhs, preferred_element_type=f32).astype(bf16)  6.85 us
    dot_general x2, matrix products, per_device(): jnp.einsum('rh,rd->hd', weighted_hidden, upstream, preferred_element_type...  6.2 us
  transfers between devices with their start and end apart: 4, of which 4 were waited for; matrix products, arithmetic and copies ran while one was open for 11% of the time, Pallas kernels for 0%

profile of v4, /device:TPU:8, one launch (start us, length us, event | category | flops | bytes accessed | tf_op | source)
XLA Modules:
  0.0 272.8 jit_solution(8301096907189134309)
XLA Ops:
  7.2 0.8 copy.53
  8.2 0.2 select_reduce_fusion
  8.5 0.8 copy.59
  9.8 0.3 convolution_convert_fusion.8
  10.1 1.2 convolution_convert_fusion.9
  11.4 0.8 concatenate.24
  12.2 0.2 squeeze.28
  12.5 17.7 %all_to_all.15 = bf16[16,2,8320]{2,1,0:T(2,128)(2,1)S(1)} all-to-all(bf16[16,2,8320]{2,1,0:T(2,128)(2,1)S(1)} %squeeze.28), channel_id=1, replica_groups=mesh['expert'=16,'dp'=16] {'expert'}, dimensions={0} | all-to-all | bytes 1064960 | tf_op jit(solution)/shard_map/all_to_all | solution.py:53
  30.1 1.0 all_gather_reshape.6
  31.2 0.2 squeeze.32
  31.4 14.0 %all_to_all.16 = bf16[16,2,8320]{2,1,0:T(2,128)(2,1)S(1)} all-to-all(bf16[16,2,8320]{2,1,0:T(2,128)(2,1)S(1)} %squeeze.32), channel_id=1, replica_groups=mesh['expert'=16,'dp'=16] {'expert'}, dimensions={0} | all-to-all | bytes 1064960 | tf_op jit(solution)/shard_map/all_to_all | solution.py:53
  45.4 1.0 all_gather_reshape.7
  46.4 0.2 reduce-scatter.2.cloned.1.call-start
  46.6 1.5 slice_bitcast_fusion.2
  48.2 0.2 fusion.30
  48.6 39.4 %all-gather.3.cloned.1.call-done = bf16[16,32,8320]{2,1,0:T(8,128)(2,1)} async-done(((bf16[1,32,8320]{2,1,0:T(8,128)(2,1)}), bf16[16,32,8320]{2,1,0:T(8,128)(2,1)}) %all-gather.3.cloned.1.call-update) | async-done | bytes 8519696 | tf_op jit(solution)/shard_map/all_gather | solution.py:55
  87.9 1.0 convert_reduce_fusion.1
  89.0 4.5 %fusion.26 = f32[512,96]{0,1:T(8,128)} fusion(bf16[512,8320]{1,0:T(8,128)(2,1)} %bitcast.78, bf16[2,96,4096]{2,1,0:T(8,128)(2,1)} %param.12), kind=kOutput, calls=%fused_computation.39 | convolution fusion | flops 402653184 | bytes 5177344 | tf_op jit(solution)/shard_map/rd,hd->rh/dot_general | solution.py:61
  93.5 51.9 %all-gather.5.cloned.1.call-done = bf16[16,32,8320]{2,1,0:T(8,128)(2,1)} async-done(((bf16[1,32,8320]{2,1,0:T(8,128)(2,1)}), bf16[16,32,8320]{2,1,0:T(8,128)(2,1)}) %all-gather.5.cloned.1.call-update) | async-done | bytes 8519696 | tf_op jit(solution)/shard_map/all_gather | solution.py:55
  145.4 4.0 %fusion.20 = f32[512,96]{0,1:T(8,128)S(1)} fusion(bf16[512,8320]{1,0:T(8,128)(2,1)} %bitcast.70, bf16[2,96,4096]{2,1,0:T(8,128)(2,1)} %param.12), kind=kOutput, calls=%fused_computation.33 | convolution fusion | flops 402653184 | bytes 5177344 | tf_op jit(solution)/shard_map/rd,hd->rh/dot_general | solution.py:61
  149.4 1.5 convert_reduce_fusion
  150.9 4.0 %fusion.10 = f32[512,96]{0,1:T(8,128)S(1)} fusion(bf16[512,8320]{1,0:T(8,128)(2,1)} %bitcast.79, bf16[2,96,4096]{2,1,0:T(8,128)(2,1)} %param.13), kind=kOutput, calls=%fused_computation.22 | convolution fusion | flops 402653184 | bytes 5177344 | tf_op jit(solution)/shard_map/rd,hd->rh/dot_general | solution.py:62
  154.9 1.4 fusion.7
  156.3 0.2 copy-done.2
  156.5 2.1 multiply_convert_fusion.5
  158.6 2.1 multiply_convert_fusion.3
  160.7 3.4 %convolution_convert_fusion.1 = bf16[512,4224]{1,0:T(8,128)(2,1)} fusion(bf16[2,4224]{1,0:T(2,128)(2,1)S(1)} %compare_convert_fusion, bf16[192,4224]{1,0:T(8,128)(2,1)S(1)} %get-tuple-element.19, bf16[512,1]{0,1:T(2,128)(2,1)S(1)} %subtract_convert_fusion.1, bf16[512,1]{0,1:T(2,128)(2,1)S(1)} %convert_element_type.167, ...), kind=kOutput, calls=%fused_computation.2 | convolution fusion | flops 845358080 | bytes 6162944 | tf_op jit(solution)/shard_map/dot_general | solution.py:80
  164.1 3.5 %convolution_convert_fusion = bf16[512,4224]{1,0:T(8,128)(2,1)} fusion(bf16[2,4224]{1,0:T(2,128)(2,1)S(1)} %compare_convert_fusion, bf16[192,4224]{1,0:T(8,128)(2,1)S(1)} %get-tuple-element.20, bf16[512,1]{0,1:T(2,128)(2,1)S(1)} %subtract_convert_fusion, bf16[512,1]{0,1:T(2,128)(2,1)S(1)} %convert_element_type.174, ...), kind=kOutput, calls=%fused_computation.1 | convolution fusion | flops 845358080 | bytes 6162944 | tf_op jit(solution)/shard_map/dot_general | solution.py:80
  167.6 7.8 %pad_maximum_fusion = bf16[16,64,4224]{2,1,0:T(8,128)(2,1)} fusion(bf16[16,32,4224]{2,1,0:T(8,128)(2,1)} %bitcast.65, bf16[16,32,4224]{2,1,0:T(8,128)(2,1)} %bitcast.64), kind=kLoop, calls=%fused_computation | loop fusion | flops 17301504 | bytes 17301504 | tf_op jit(solution)/shard_map/concatenate | solution.py:94
  175.5 0.8 copy-done.7
  176.3 3.0 %fusion = bf16[1,96,4096]{2,1,0:T(8,128)(2,1)S(1)} fusion(bf16[512,96]{0,1:T(8,128)(2,1)S(1)} %copy-done.7, bf16[512,8320]{1,0:T(8,128)(2,1)} %bitcast.80), kind=kOutput, calls=%fused_computation.9 | convolution fusion | flops 403046400 | bytes 5079040 | tf_op jit(solution)/shard_map/rh,rd->hd/dot_general | solution.py:83
  179.3 3.0 %fusion.2 = bf16[1,96,4096]{2,1,0:T(8,128)(2,1)S(1)} fusion(bf16[512,96]{0,1:T(8,128)(2,1)S(1)} %get-tuple-element.15, bf16[512,8320]{1,0:T(8,128)(2,1)} %bitcast.81), kind=kOutput, calls=%fused_computation.11 | convolution fusion | flops 403046400 | bytes 5079040 | tf_op jit(solution)/shard_map/rh,rd->hd/dot_general | solution.py:86
  182.4 3.0 %fusion.1 = bf16[1,96,4096]{2,1,0:T(8,128)(2,1)S(1)} fusion(bf16[512,96]{0,1:T(8,128)(2,1)S(1)} %copy-done.11, bf16[512,8320]{1,0:T(8,128)(2,1)} %bitcast.72), kind=kOutput, calls=%fused_computation.10 | convolution fusion | flops 403046400 | bytes 5079040 | tf_op jit(solution)/shard_map/rh,rd->hd/dot_general | solution.py:83
  185.4 3.1 %fusion.3 = bf16[1,96,4096]{2,1,0:T(8,128)(2,1)S(1)} fusion(bf16[512,96]{0,1:T(8,128)(2,1)S(1)} %copy-done.9, bf16[512,8320]{1,0:T(8,128)(2,1)} %bitcast.73), kind=kOutput, calls=%fused_computation.12 | convolution fusion | flops 403046400 | bytes 5079040 | tf_op jit(solution)/shard_map/rh,rd->hd/dot_general | solution.py:86
  188.5 3.2 %fusion.4 = bf16[1,96,4096]{2,1,0:T(8,128)(2,1)S(1)} fusion(bf16[512,8320]{1,0:T(8,128)(2,1)} %bitcast.82, f32[512]{0:T(512)S(1)} %convert_reduce_fusion.1, f32[512,96]{0,1:T(8,128)S(1)} %copy-done.16, f32[512,96]{0,1:T(8,128)S(1)} %copy-done.17), kind=kOutput, calls=%fused_computation.13 | convolution fusion | flops 403390464 | bytes 5376000 | tf_op jit(solution)/shard_map/rh,rd->hd/dot_general | solution.py:89
  191.8 1.9 pad_maximum_fusion.5
  193.7 51.7 %reduce-scatter.2.cloned.1.call-done = bf16[1,64,4224]{2,1,0:T(8,128)(2,1)} async-done(((bf16[16,64,4224]{2,1,0:T(8,128)(2,1)}), bf16[1,64,4224]{2,1,0:T(8,128)(2,1)}) %reduce-scatter.2.cloned.1.call-update) | async-done | bytes 540688 | tf_op jit(solution)/shard_map/reduce_scatter | solution.py:94
  245.4 1.2 reshape.179
  246.6 1.2 copy.61
  247.8 7.3 %all-to-all-start.2 = ((bf16[2,16,2,4224]{3,2,0,1:T(2,128)(2,1)}), bf16[2,16,2,4224]{3,2,0,1:T(2,128)(2,1)S(1)}, u32[]{:S(2)}, u32[]{:S(2)}) async-start(bf16[2,16,2,4224]{3,2,0,1:T(2,128)(2,1)} %copy.61), calls=%async_computation.3 | async-start | bytes 1081344 | tf_op jit(solution)/shard_map/all_to_all | solution.py:96
  255.1 3.0 %fusion.5 = bf16[1,96,4096]{2,1,0:T(8,128)(2,1)S(1)} fusion(bf16[512,8320]{1,0:T(8,128)(2,1)} %bitcast.74, f32[512]{0:T(512)S(1)} %convert_reduce_fusion, f32[512,96]{0,1:T(8,128)S(1)} %copy-done.13, f32[512,96]{0,1:T(8,128)S(1)} %copy-done.14), kind=kOutput, calls=%fused_computation.14 | convolution fusion | flops 403390464 | bytes 5376000 | tf_op jit(solution)/shard_map/rh,rd->hd/dot_general | solution.py:89
  258.1 1.3 pad_maximum_fusion.7
  259.4 4.5 %all-to-all-done.2 = bf16[2,16,2,4224]{3,2,0,1:T(2,128)(2,1)S(1)} async-done(((bf16[2,16,2,4224]{3,2,0,1:T(2,128)(2,1)}), bf16[2,16,2,4224]{3,2,0,1:T(2,128)(2,1)S(1)}, u32[]{:S(2)}, u32[]{:S(2)}) %all-to-all-start.2) | async-done | bytes 540704 | tf_op jit(solution)/shard_map/all_to_all | solution.py:96
  263.9 0.4 copy.62
  264.3 0.2 reshape.180
  264.5 0.8 convolution_convert_fusion.10
  265.3 0.2 add_reduce_fusion
  265.5 0.8 fusion.61
  (61 shorter events, 1.4 us)
Async XLA Ops:
  7.2 2.6 copy-start
  7.2 80.8 %all-gather.3.cloned.1.call-start = ((), (), s32[]{:S(2)}) async-start(), calls=%async_computation.4 | async-start | bytes 9052160 | tf_op jit(solution)/shard_map/all_gather | solution.py:55
  31.1 114.3 %all-gather.5.cloned.1.call-start = ((), (), s32[]{:S(2)}) async-start(), calls=%async_computation.5 | async-start | bytes 9052160 | tf_op jit(solution)/shard_map/all_gather | solution.py:55
  31.2 16.9 %copy-start.1 = (bf16[2,96,4096]{2,1,0:T(8,128)(2,1)S(1)}, bf16[2,96,4096]{2,1,0:T(8,128)(2,1)}, u32[]{:S(2)}) copy-start(bf16[2,96,4096]{2,1,0:T(8,128)(2,1)} %param.12) | copy-start | bytes 4718596
  46.4 199.0 %reduce-scatter.2.cloned.1.call-start = ((), (), s32[]{:S(2)}) async-start(), calls=%async_computation.6 | async-start | bytes 9191424 | tf_op jit(solution)/shard_map/reduce_scatter | solution.py:94
  145.4 9.4 %copy-start.3 = (bf16[16,32,8320]{2,1,0:T(8,128)(2,1)S(1)}, bf16[16,32,8320]{2,1,0:T(8,128)(2,1)}, u32[]{:S(2)}) copy-start(bf16[16,32,8320]{2,1,0:T(8,128)(2,1)} %all-gather.5.cloned.1.call-done) | copy-start | bytes 25559044
  145.4 9.5 %copy-start.5 = (bf16[2,96,4096]{2,1,0:T(8,128)(2,1)S(1)}, bf16[2,96,4096]{2,1,0:T(8,128)(2,1)}, u32[]{:S(2)}) copy-start(bf16[2,96,4096]{2,1,0:T(8,128)(2,1)} %param.13) | copy-start | bytes 4718596
  149.4 9.2 %copy-start.12 = (f32[512,96]{0,1:T(8,128)}, f32[512,96]{0,1:T(8,128)S(1)}, u32[]{:S(2)}) copy-start(f32[512,96]{0,1:T(8,128)S(1)} %fusion.20) | copy-start | bytes 589828
  150.8 5.4 %copy-start.4 = (bf16[16,32,8320]{2,1,0:T(8,128)(2,1)S(1)}, bf16[16,32,8320]{2,1,0:T(8,128)(2,1)}, u32[]{:S(2)}) copy-start(bf16[16,32,8320]{2,1,0:T(8,128)(2,1)} %all-gather.3.cloned.1.call-done) | copy-start | bytes 25559044
  154.8 1.6 copy-start.2
  154.9 1.6 copy-start.15
  158.6 2.1 copy-start.6
  160.7 6.9 %copy-start.8 = (bf16[512,96]{0,1:T(8,128)(2,1)}, bf16[512,96]{0,1:T(8,128)(2,1)S(1)}, u32[]{:S(2)}) copy-start(bf16[512,96]{0,1:T(8,128)(2,1)S(1)} %get-tuple-element.16) | copy-start | bytes 294916
  160.7 6.9 %copy-start.10 = (bf16[512,96]{0,1:T(8,128)(2,1)}, bf16[512,96]{0,1:T(8,128)(2,1)S(1)}, u32[]{:S(2)}) copy-start(bf16[512,96]{0,1:T(8,128)(2,1)S(1)} %get-tuple-element.13) | copy-start | bytes 294916
  175.4 0.9 copy-start.7
  179.3 3.1 %copy-start.11 = (bf16[512,96]{0,1:T(8,128)(2,1)S(1)}, bf16[512,96]{0,1:T(8,128)(2,1)}, u32[]{:S(2)}) copy-start(bf16[512,96]{0,1:T(8,128)(2,1)} %copy-done.10) | copy-start | bytes 294916
  182.3 3.0 %copy-start.9 = (bf16[512,96]{0,1:T(8,128)(2,1)S(1)}, bf16[512,96]{0,1:T(8,128)(2,1)}, u32[]{:S(2)}) copy-start(bf16[512,96]{0,1:T(8,128)(2,1)} %copy-done.8) | copy-start | bytes 294916
  185.4 3.1 %copy-start.16 = (f32[512,96]{0,1:T(8,128)S(1)}, f32[512,96]{0,1:T(8,128)}, u32[]{:S(2)}) copy-start(f32[512,96]{0,1:T(8,128)} %fusion.26) | copy-start | bytes 589828
  185.4 3.1 %copy-start.17 = (f32[512,96]{0,1:T(8,128)S(1)}, f32[512,96]{0,1:T(8,128)}, u32[]{:S(2)}) copy-start(f32[512,96]{0,1:T(8,128)} %get-tuple-element.18) | copy-start | bytes 589828
  191.7 63.3 %copy-start.13 = (f32[512,96]{0,1:T(8,128)S(1)}, f32[512,96]{0,1:T(8,128)}, u32[]{:S(2)}) copy-start(f32[512,96]{0,1:T(8,128)} %copy-done.12) | copy-start | bytes 589828
  191.7 63.3 %copy-start.14 = (f32[512,96]{0,1:T(8,128)S(1)}, f32[512,96]{0,1:T(8,128)}, u32[]{:S(2)}) copy-start(f32[512,96]{0,1:T(8,128)} %get-tuple-element.17) | copy-start | bytes 589828
  247.8 16.1 %all-to-all-start.2 = ((bf16[2,16,2,4224]{3,2,0,1:T(2,128)(2,1)}), bf16[2,16,2,4224]{3,2,0,1:T(2,128)(2,1)S(1)}, u32[]{:S(2)}, u32[]{:S(2)}) async-start(bf16[2,16,2,4224]{3,2,0,1:T(2,128)(2,1)} %copy.61), calls=%async_computation.3 | async-start | bytes 1081344 | tf_op jit(solution)/shard_map/all_to_all | solution.py:96
Sparse Core Ops, SparseCore 0:
  31.3 56.6 all-gather.2
  90.3 55.0 all-gather.4
  175.5 69.8 reduce-scatter.1

commit v5 on v4

--- a/solution.py
+++ b/solution.py
@@ -48,7 +48,7 @@
         jnp.arange(back_width, dtype=jnp.int32)[None, :]
         == model_width + jnp.arange(2, dtype=jnp.int32)[:, None]
     ).astype(bf16)
-    backs, ggw, guw, gdw = [], [], [], []
+    ggw, guw, gdw = [], [], []
     for l in range(local_experts):
         blk = lax.all_to_all(payload[l], "expert", split_axis=0, concat_axis=0, tiled=True)
         blk = blk.reshape(block_rows, width)
@@ -78,7 +78,11 @@
         stacked = jnp.pad(jnp.concatenate([gw, uw], axis=0), ((0, 0), (0, PAD)))
         rhs = jnp.concatenate([stacked, extra_rows], axis=0)
         back = jnp.dot(lhs, rhs, preferred_element_type=f32).astype(bf16)
-        backs.append(back.reshape(n_dp, block_rows, back_width))
+        back = back.reshape(n_dp, block_rows, back_width)
+        if l == 0:
+            merged = lax.optimization_barrier(jnp.pad(back, ((0, 0), (0, (local_experts - 1) * block_rows), (0, 0))))
+        else:
+            merged = lax.dynamic_update_slice_in_dim(merged, back, l * block_rows, axis=1)
         ggw.append(
             jnp.einsum("rh,rd->hd", grad_gate_pre, inputs, preferred_element_type=f32).astype(bf16)
         )
@@ -91,7 +95,7 @@
             )
         )
 
-    back = lax.psum_scatter(jnp.concatenate(backs, axis=1), "dp", scatter_dimension=0, tiled=True)
+    back = lax.psum_scatter(merged, "dp", scatter_dimension=0, tiled=True)
     back = back.reshape(local_experts, groups, capacity, back_width)
     returned = lax.all_to_all(back, "expert", split_axis=1, concat_axis=1, tiled=True)
     returned = returned.reshape(slot_count, back_width)

time: 273 us -> 268 us (0.982)
  other arithmetic: 14.5 us -> 6.73 us
  local copies, waits for them, and re-layouts: 10.9 us -> 17.7 us
  matrix products: 46.5 us -> 42.5 us
    concatenate x1 -> x0, other arithmetic: 7.8 us -> none  [per_device(): jnp.concatenate(backs, axis=1)]
    pad x0 -> x1, local copies, waits for them, and re-layouts: none -> 4.47 us  [per_device(): jnp.pad(back, ((0, 0), (0, (local_experts - 1) * block_rows), (0, 0)))]
    dot_general x2, matrix products: 6.85 us -> 2.79 us  [per_device(): back = jnp.dot(lhs, rhs, preferred_element_type=f32).astype(bf16)]
where the time goes in v5:
time: 268 us
  waiting for transfers between devices  147 us (55%)
  matrix products  42.5 us (16%)
  blocking collectives  31.6 us (12%)
  local copies, waits for them, and re-layouts  17.7 us (7%)
  between operations  14.1 us (5%)
  starting transfers between devices  7.56 us (3%)
  other arithmetic  6.73 us (3%)
    all_gather x2, waiting for transfers between devices, per_device(): rows = lax.all_gather(blk, 'dp', axis=0).reshape(gathered_rows, width)  91.3 us
    reduce_scatter x1, waiting for transfers between devices, per_device(): back = lax.psum_scatter(merged, 'dp', scatter_dimension=0, tiled=True)  51.6 us
    all_to_all x2, blocking collectives, per_device(): lax.all_to_all(payload[l], 'expert', split_axis=0, concat_axis=0, tiled=T...  31.6 us
    dot_general x2, matrix products, per_device(): up_pre = jnp.einsum('rd,hd->rh', inputs, uw, preferred_element_type=f32)  8.46 us
    all_to_all x1, starting transfers between devices, per_device(): lax.all_to_all(back, 'expert', split_axis=1, concat_axis=1, tiled=True)  7.26 us
    dot_general x2, matrix products, per_device(): jnp.einsum('rh,rd->hd', weighted_hidden, upstream, preferred_element_type...  6.21 us
    dot_general x2, matrix products, per_device(): jnp.einsum('rh,rd->hd', grad_up_pre, inputs, preferred_element_type=f32)  6.19 us
    dot_general x2, matrix products, per_device(): jnp.einsum('rh,rd->hd', grad_gate_pre, inputs, preferred_element_type=f32)  6.05 us
  transfers between devices with their start and end apart: 4, of which 4 were waited for; matrix products, arithmetic and copies ran while one was open for 11% of the time, Pallas kernels for 0%

profile of v5, /device:TPU:8, one launch (start us, length us, event | category | flops | bytes accessed | tf_op | source)
XLA Modules:
  0.0 267.7 jit_solution(14746488628512600555)
XLA Ops:
  7.2 0.8 copy.53
  8.2 0.2 select_reduce_fusion
  8.5 0.8 copy.59
  9.8 0.3 convolution_convert_fusion.8
  10.1 1.2 convolution_convert_fusion.9
  11.4 0.8 concatenate.21
  12.2 0.2 squeeze.32
  12.5 17.7 %all_to_all.15 = bf16[16,2,8320]{2,1,0:T(2,128)(2,1)S(1)} all-to-all(bf16[16,2,8320]{2,1,0:T(2,128)(2,1)S(1)} %squeeze.32), channel_id=1, replica_groups=mesh['expert'=16,'dp'=16] {'expert'}, dimensions={0} | all-to-all | bytes 1064960 | tf_op jit(solution)/shard_map/all_to_all | solution.py:53
  30.1 1.0 all_gather_reshape.7
  31.2 0.2 squeeze.28
  31.4 14.0 %all_to_all.16 = bf16[16,2,8320]{2,1,0:T(2,128)(2,1)S(1)} all-to-all(bf16[16,2,8320]{2,1,0:T(2,128)(2,1)S(1)} %squeeze.28), channel_id=1, replica_groups=mesh['expert'=16,'dp'=16] {'expert'}, dimensions={0} | all-to-all | bytes 1064960 | tf_op jit(solution)/shard_map/all_to_all | solution.py:53
  45.4 1.0 all_gather_reshape.6
  46.4 0.2 reduce-scatter.2.cloned.1.call-start
  46.6 1.5 slice_bitcast_fusion
  48.2 0.2 fusion.30
  48.6 39.4 %all-gather.5.cloned.1.call-done = bf16[16,32,8320]{2,1,0:T(8,128)(2,1)} async-done(((bf16[1,32,8320]{2,1,0:T(8,128)(2,1)}), bf16[16,32,8320]{2,1,0:T(8,128)(2,1)}) %all-gather.5.cloned.1.call-update) | async-done | bytes 8519696 | tf_op jit(solution)/shard_map/all_gather | solution.py:55
  87.9 1.0 convert_reduce_fusion
  89.0 4.5 %fusion.20 = f32[512,96]{0,1:T(8,128)} fusion(bf16[512,8320]{1,0:T(8,128)(2,1)} %bitcast.78, bf16[2,96,4096]{2,1,0:T(8,128)(2,1)} %param.12), kind=kOutput, calls=%fused_computation.32 | convolution fusion | flops 402653184 | bytes 5177344 | tf_op jit(solution)/shard_map/rd,hd->rh/dot_general | solution.py:61
  93.5 51.9 %all-gather.3.cloned.1.call-done = bf16[16,32,8320]{2,1,0:T(8,128)(2,1)} async-done(((bf16[1,32,8320]{2,1,0:T(8,128)(2,1)}), bf16[16,32,8320]{2,1,0:T(8,128)(2,1)}) %all-gather.3.cloned.1.call-update) | async-done | bytes 8519696 | tf_op jit(solution)/shard_map/all_gather | solution.py:55
  145.4 4.0 %fusion.26 = f32[512,96]{0,1:T(8,128)S(1)} fusion(bf16[512,8320]{1,0:T(8,128)(2,1)} %bitcast.70, bf16[2,96,4096]{2,1,0:T(8,128)(2,1)} %param.12), kind=kOutput, calls=%fused_computation.38 | convolution fusion | flops 402653184 | bytes 5177344 | tf_op jit(solution)/shard_map/rd,hd->rh/dot_general | solution.py:61
  149.4 1.5 convert_reduce_fusion.1
  150.9 4.0 %fusion.7 = f32[512,96]{0,1:T(8,128)S(1)} fusion(bf16[512,8320]{1,0:T(8,128)(2,1)} %bitcast.79, bf16[2,96,4096]{2,1,0:T(8,128)(2,1)} %param.13), kind=kOutput, calls=%fused_computation.18 | convolution fusion | flops 402653184 | bytes 5177344 | tf_op jit(solution)/shard_map/rd,hd->rh/dot_general | solution.py:62
  154.9 1.4 fusion.10
  156.3 0.2 copy-done.2
  156.5 2.1 multiply_convert_fusion.3
  158.6 2.1 multiply_convert_fusion.5
  160.7 1.4 convolution_convert_fusion.1
  162.1 4.5 %pad.12 = bf16[16,64,4224]{2,1,0:T(8,128)(2,1)} pad(bf16[16,32,4224]{2,1,0:T(8,128)(2,1)S(1)} %bitcast.64, bf16[]{:T(256)} %constant.41.clone.1), padding=0_0x0_32x0_0 | pad | bytes 12976130 | tf_op jit(solution)/shard_map/jit(_pad)/pad | solution.py:83
  166.6 1.4 convolution_convert_fusion
  168.0 2.3 constant_dynamic-update-slice_fusion
  170.4 0.8 copy-done.7
  171.2 3.0 %fusion.1 = bf16[1,96,4096]{2,1,0:T(8,128)(2,1)S(1)} fusion(bf16[512,96]{0,1:T(8,128)(2,1)S(1)} %copy-done.7, bf16[512,8320]{1,0:T(8,128)(2,1)} %bitcast.80), kind=kOutput, calls=%fused_computation.9 | convolution fusion | flops 403046400 | bytes 5079040 | tf_op jit(solution)/shard_map/rh,rd->hd/dot_general | solution.py:87
  174.2 3.1 %fusion.3 = bf16[1,96,4096]{2,1,0:T(8,128)(2,1)S(1)} fusion(bf16[512,96]{0,1:T(8,128)(2,1)S(1)} %get-tuple-element.15, bf16[512,8320]{1,0:T(8,128)(2,1)} %bitcast.81), kind=kOutput, calls=%fused_computation.11 | convolution fusion | flops 403046400 | bytes 5079040 | tf_op jit(solution)/shard_map/rh,rd->hd/dot_general | solution.py:90
  177.3 3.1 %fusion = bf16[1,96,4096]{2,1,0:T(8,128)(2,1)S(1)} fusion(bf16[512,96]{0,1:T(8,128)(2,1)S(1)} %copy-done.11, bf16[512,8320]{1,0:T(8,128)(2,1)} %bitcast.72), kind=kOutput, calls=%fused_computation.8 | convolution fusion | flops 403046400 | bytes 5079040 | tf_op jit(solution)/shard_map/rh,rd->hd/dot_general | solution.py:87
  180.4 3.1 %fusion.2 = bf16[1,96,4096]{2,1,0:T(8,128)(2,1)S(1)} fusion(bf16[512,96]{0,1:T(8,128)(2,1)S(1)} %copy-done.9, bf16[512,8320]{1,0:T(8,128)(2,1)} %bitcast.73), kind=kOutput, calls=%fused_computation.10 | convolution fusion | flops 403046400 | bytes 5079040 | tf_op jit(solution)/shard_map/rh,rd->hd/dot_general | solution.py:90
  183.5 3.2 %fusion.5 = bf16[1,96,4096]{2,1,0:T(8,128)(2,1)S(1)} fusion(bf16[512,8320]{1,0:T(8,128)(2,1)} %bitcast.82, f32[512]{0:T(512)S(1)} %convert_reduce_fusion, f32[512,96]{0,1:T(8,128)S(1)} %copy-done.16, f32[512,96]{0,1:T(8,128)S(1)} %copy-done.17), kind=kOutput, calls=%fused_computation.13 | convolution fusion | flops 403390464 | bytes 5376000 | tf_op jit(solution)/shard_map/rh,rd->hd/dot_general | solution.py:93
  186.8 1.9 pad_maximum_fusion.4
  188.7 51.6 %reduce-scatter.2.cloned.1.call-done = bf16[1,64,4224]{2,1,0:T(8,128)(2,1)} async-done(((bf16[16,64,4224]{2,1,0:T(8,128)(2,1)}), bf16[1,64,4224]{2,1,0:T(8,128)(2,1)}) %reduce-scatter.2.cloned.1.call-update) | async-done | bytes 540688 | tf_op jit(solution)/shard_map/reduce_scatter | solution.py:98
  240.3 1.2 reshape.179
  241.6 1.2 copy.61
  242.8 7.3 %all-to-all-start.2 = ((bf16[2,16,2,4224]{3,2,0,1:T(2,128)(2,1)}), bf16[2,16,2,4224]{3,2,0,1:T(2,128)(2,1)S(1)}, u32[]{:S(2)}, u32[]{:S(2)}) async-start(bf16[2,16,2,4224]{3,2,0,1:T(2,128)(2,1)} %copy.61), calls=%async_computation.3 | async-start | bytes 1081344 | tf_op jit(solution)/shard_map/all_to_all | solution.py:100
  250.0 3.0 %fusion.4 = bf16[1,96,4096]{2,1,0:T(8,128)(2,1)S(1)} fusion(bf16[512,8320]{1,0:T(8,128)(2,1)} %bitcast.74, f32[512]{0:T(512)S(1)} %convert_reduce_fusion.1, f32[512,96]{0,1:T(8,128)S(1)} %copy-done.13, f32[512,96]{0,1:T(8,128)S(1)} %copy-done.14), kind=kOutput, calls=%fused_computation.12 | convolution fusion | flops 403390464 | bytes 5376000 | tf_op jit(solution)/shard_map/rh,rd->hd/dot_general | solution.py:93
  253.0 1.3 pad_maximum_fusion.6
  254.3 4.5 %all-to-all-done.2 = bf16[2,16,2,4224]{3,2,0,1:T(2,128)(2,1)S(1)} async-done(((bf16[2,16,2,4224]{3,2,0,1:T(2,128)(2,1)}), bf16[2,16,2,4224]{3,2,0,1:T(2,128)(2,1)S(1)}, u32[]{:S(2)}, u32[]{:S(2)}) %all-to-all-start.2) | async-done | bytes 540704 | tf_op jit(solution)/shard_map/all_to_all | solution.py:100
  258.8 0.4 copy.62
  259.2 0.2 reshape.180
  259.4 0.8 convolution_convert_fusion.10
  260.4 0.8 fusion.61
  (62 shorter events, 1.6 us)
Async XLA Ops:
  7.2 2.6 copy-start
  7.2 80.8 %all-gather.5.cloned.1.call-start = ((), (), s32[]{:S(2)}) async-start(), calls=%async_computation.5 | async-start | bytes 9052160 | tf_op jit(solution)/shard_map/all_gather | solution.py:55
  31.1 114.3 %all-gather.3.cloned.1.call-start = ((), (), s32[]{:S(2)}) async-start(), calls=%async_computation.4 | async-start | bytes 9052160 | tf_op jit(solution)/shard_map/all_gather | solution.py:55
  31.2 16.9 %copy-start.1 = (bf16[2,96,4096]{2,1,0:T(8,128)(2,1)S(1)}, bf16[2,96,4096]{2,1,0:T(8,128)(2,1)}, u32[]{:S(2)}) copy-start(bf16[2,96,4096]{2,1,0:T(8,128)(2,1)} %param.12) | copy-start | bytes 4718596
  46.4 193.9 %reduce-scatter.2.cloned.1.call-start = ((), (), s32[]{:S(2)}) async-start(), calls=%async_computation.6 | async-start | bytes 9191424 | tf_op jit(solution)/shard_map/reduce_scatter | solution.py:98
  145.4 9.4 %copy-start.3 = (bf16[16,32,8320]{2,1,0:T(8,128)(2,1)S(1)}, bf16[16,32,8320]{2,1,0:T(8,128)(2,1)}, u32[]{:S(2)}) copy-start(bf16[16,32,8320]{2,1,0:T(8,128)(2,1)} %all-gather.3.cloned.1.call-done) | copy-start | bytes 25559044
  145.4 9.5 %copy-start.5 = (bf16[2,96,4096]{2,1,0:T(8,128)(2,1)S(1)}, bf16[2,96,4096]{2,1,0:T(8,128)(2,1)}, u32[]{:S(2)}) copy-start(bf16[2,96,4096]{2,1,0:T(8,128)(2,1)} %param.13) | copy-start | bytes 4718596
  149.4 9.2 %copy-start.12 = (f32[512,96]{0,1:T(8,128)}, f32[512,96]{0,1:T(8,128)S(1)}, u32[]{:S(2)}) copy-start(f32[512,96]{0,1:T(8,128)S(1)} %fusion.26) | copy-start | bytes 589828
  150.8 5.4 %copy-start.4 = (bf16[16,32,8320]{2,1,0:T(8,128)(2,1)S(1)}, bf16[16,32,8320]{2,1,0:T(8,128)(2,1)}, u32[]{:S(2)}) copy-start(bf16[16,32,8320]{2,1,0:T(8,128)(2,1)} %all-gather.5.cloned.1.call-done) | copy-start | bytes 25559044
  154.8 1.6 copy-start.2
  154.9 1.6 copy-start.15
  158.6 8.0 %copy-start.6 = (bf16[512,96]{0,1:T(8,128)(2,1)}, bf16[512,96]{0,1:T(8,128)(2,1)S(1)}, u32[]{:S(2)}) copy-start(bf16[512,96]{0,1:T(8,128)(2,1)S(1)} %get-tuple-element.11) | copy-start | bytes 294916
  160.7 5.9 %copy-start.8 = (bf16[512,96]{0,1:T(8,128)(2,1)}, bf16[512,96]{0,1:T(8,128)(2,1)S(1)}, u32[]{:S(2)}) copy-start(bf16[512,96]{0,1:T(8,128)(2,1)S(1)} %get-tuple-element.16) | copy-start | bytes 294916
  160.7 5.9 %copy-start.10 = (bf16[512,96]{0,1:T(8,128)(2,1)}, bf16[512,96]{0,1:T(8,128)(2,1)S(1)}, u32[]{:S(2)}) copy-start(bf16[512,96]{0,1:T(8,128)(2,1)S(1)} %get-tuple-element.13) | copy-start | bytes 294916
  170.3 0.9 copy-start.7
  174.2 3.1 %copy-start.11 = (bf16[512,96]{0,1:T(8,128)(2,1)S(1)}, bf16[512,96]{0,1:T(8,128)(2,1)}, u32[]{:S(2)}) copy-start(bf16[512,96]{0,1:T(8,128)(2,1)} %copy-done.10) | copy-start | bytes 294916
  177.3 3.1 %copy-start.9 = (bf16[512,96]{0,1:T(8,128)(2,1)S(1)}, bf16[512,96]{0,1:T(8,128)(2,1)}, u32[]{:S(2)}) copy-start(bf16[512,96]{0,1:T(8,128)(2,1)} %copy-done.8) | copy-start | bytes 294916
  180.4 3.2 %copy-start.16 = (f32[512,96]{0,1:T(8,128)S(1)}, f32[512,96]{0,1:T(8,128)}, u32[]{:S(2)}) copy-start(f32[512,96]{0,1:T(8,128)} %fusion.20) | copy-start | bytes 589828
  180.4 3.2 %copy-start.17 = (f32[512,96]{0,1:T(8,128)S(1)}, f32[512,96]{0,1:T(8,128)}, u32[]{:S(2)}) copy-start(f32[512,96]{0,1:T(8,128)} %get-tuple-element.18) | copy-start | bytes 589828
  186.7 63.3 %copy-start.13 = (f32[512,96]{0,1:T(8,128)S(1)}, f32[512,96]{0,1:T(8,128)}, u32[]{:S(2)}) copy-start(f32[512,96]{0,1:T(8,128)} %copy-done.12) | copy-start | bytes 589828
  186.8 63.3 %copy-start.14 = (f32[512,96]{0,1:T(8,128)S(1)}, f32[512,96]{0,1:T(8,128)}, u32[]{:S(2)}) copy-start(f32[512,96]{0,1:T(8,128)} %get-tuple-element.17) | copy-start | bytes 589828
  242.8 16.1 %all-to-all-start.2 = ((bf16[2,16,2,4224]{3,2,0,1:T(2,128)(2,1)}), bf16[2,16,2,4224]{3,2,0,1:T(2,128)(2,1)S(1)}, u32[]{:S(2)}, u32[]{:S(2)}) async-start(bf16[2,16,2,4224]{3,2,0,1:T(2,128)(2,1)} %copy.61), calls=%async_computation.3 | async-start | bytes 1081344 | tf_op jit(solution)/shard_map/all_to_all | solution.py:100
Sparse Core Ops, SparseCore 0:
  31.3 56.6 all-gather.4
  90.3 55.0 all-gather.2
  170.5 69.8 reduce-scatter.1
